TPU v7x, 128 devices: a whole 4x4x4 slice. The times are simulated.
128 devices in a mesh: dp: 16 (over x, y), head: 8 (over z, core).
Axes of the slice: x: 4, y: 4, z: 4, core: 2. Of those that a mesh axis runs over, the one named last changes fastest.
Arguments:
- tokens: bfloat16 [16384, 2048], P(('dp', 'head')), may hold values from -6 to 6
- cached_lens: int32 [16], replicated, may hold values from 1 to 2048, as said below
- latent_cache: bfloat16 [16, 2048, 576], P(None, 'dp'), may hold values from -720 to 720
- attn_gain: float32 [2048], replicated, may hold values from 0.1 to 1.9
- q_weight: bfloat16 [2048, 3072], P(None, 'head'), may hold values from -0.125 to 0.125
- kv_down: bfloat16 [2048, 576], replicated, may hold values from -0.125 to 0.125
- latent_gain: float32 [512], replicated, may hold values from 0.1 to 1.9
- kv_up: bfloat16 [512, 4096], P(None, 'head'), may hold values from -1 to 1
- o_weight: bfloat16 [2048, 2048], P('head'), may hold values from -0.125 to 0.125
- moe_gain: float32 [2048], replicated, may hold values from 0.1 to 1.9
- routes: int32 [16384, 6], P(('dp', 'head')), may hold values from 0 to 63, all different within a row; in each aligned block of 128 rows (0 to 127, 128 to 255, ...) at most 16 rows name the same one
- route_weights: float32 [16384, 6], P(('dp', 'head')), may hold values from 0.1 to 1
- expert_gate_up: bfloat16 [128, 2048, 1408], P(('dp', 'head')), may hold values from -0.125 to 0.125
- expert_down: bfloat16 [128, 704, 2048], P(('dp', 'head')), may hold values from -0.15625 to 0.15625
Outputs:
- layer_out: bfloat16 [16384, 2048], P(('dp', 'head'))
Inputs may be any that keep to these rules, and one draw needn't show every extreme that they name: `cached_lens`: one request's cached length is exactly 2048. `routes`: each token names 6 different experts; among the rows of one device (aligned blocks of 128 tokens) no expert is named more than 16 times, a bound that some block reaches.
All inputs are finite; a program needn't handle non-finite values.
Results may differ from a plain program's by a relative error of at most 0.019.
The roundings to bfloat16 on the way count: a program that leaves them out, or rounds other values in their place, can miss the bound.
Values may be sent and summed in bfloat16 or wider, within the bound.
No kernel may reach another device: no remote copies, remote signals or barrier semaphores. Data moves between devices by JAX's collectives and lax.ppermute only.
A program may use at most 128 MiB of HBM per device.

v0:
```python
import jax
import jax.numpy as jnp
import numpy as np
from jax import lax
from jax.sharding import PartitionSpec as P

D = 2048
HN = 128
HR = 64
HV = 128
LAT = 512
EXPERTS = 64
TOPK = 6
CACHE = 2048
CAP = 16
HALF = 704
HEAD = ("z", "core")
ROWS = ("dp", "z", "core")


NORM_EPS = 1e-06


def norm_rows(values, gain_row):
    return (
        values * lax.rsqrt(jnp.mean(values * values, axis=-1, keepdims=True) + NORM_EPS) * gain_row
    )


def angle_table(positions):
    half_width = HR // 2
    inverse = np.exp(np.arange(half_width) * (-np.log(10000.0) / half_width)).astype(np.float32)
    return positions.astype(jnp.float32)[:, None] * jnp.asarray(inverse, dtype=jnp.float32)[None, :]


def rotate_pair(values, angles):
    half_width = values.shape[-1] // 2
    cosine = jnp.cos(angles)
    sine_part = jnp.sin(angles)
    former = values[..., :half_width]
    latter = values[..., half_width:]
    return jnp.concatenate(
        [former * cosine - latter * sine_part, latter * cosine + former * sine_part], axis=-1
    )


def query_rows(normed, q_weight, positions):
    mixed_rows = jnp.dot(normed, q_weight, preferred_element_type=jnp.float32)
    head_count = q_weight.shape[1] // (HN + HR)
    mixed_rows = mixed_rows.reshape(normed.shape[0], head_count, HN + HR)
    turned = rotate_pair(mixed_rows[:, :, HN:], angle_table(positions)[:, None, :])
    joined = jnp.concatenate([mixed_rows[:, :, :HN], turned], axis=2)
    return joined.reshape(normed.shape[0], head_count * (HN + HR)).astype(jnp.bfloat16)


def fresh_rows(normed, kv_down, latent_gain, positions):
    mixed_rows = jnp.dot(normed, kv_down, preferred_element_type=jnp.float32)
    latent = norm_rows(mixed_rows[:, :LAT], latent_gain)
    turned = rotate_pair(mixed_rows[:, LAT:], angle_table(positions))
    return jnp.concatenate([latent, turned], axis=1).astype(jnp.bfloat16)


def expand_rows(key_rows, kv_up):
    return jnp.dot(key_rows[:, :LAT], kv_up, preferred_element_type=jnp.float32).astype(
        jnp.bfloat16
    )


def attend(block_q, key_wide, rope_keys, visible, head_count):
    query_heads = block_q.reshape(block_q.shape[0], head_count, HN + HR)
    key_heads = key_wide.reshape(key_wide.shape[0], head_count, HN + HV)
    scores = jnp.einsum(
        "qhd,khd->hqk",
        query_heads[:, :, :HN],
        key_heads[:, :, :HN],
        preferred_element_type=jnp.float32,
    )
    scores = scores + jnp.einsum(
        "qhd,kd->hqk", query_heads[:, :, HN:], rope_keys, preferred_element_type=jnp.float32
    )
    scores = scores * (HN + HR) ** (-0.5)
    scores = jnp.where(visible[None], scores, -1e30)
    row_max = jnp.max(scores, axis=2, keepdims=True)
    weights = jnp.where(visible[None], jnp.exp(scores - row_max), 0.0)
    prob_rows = (weights / jnp.sum(weights, axis=2, keepdims=True)).astype(jnp.bfloat16)
    mixed_rows = jnp.einsum(
        "hqk,khd->qhd", prob_rows, key_heads[:, :, HN:], preferred_element_type=jnp.float32
    )
    return mixed_rows.astype(jnp.bfloat16)


def expert_half(rows, gate_up, down):
    mixed_rows = jnp.dot(rows, gate_up, preferred_element_type=jnp.float32)
    active = (jax.nn.silu(mixed_rows[:, :HALF]) * mixed_rows[:, HALF:]).astype(jnp.bfloat16)
    return (
        jnp.dot(active, down, preferred_element_type=jnp.float32)
        .astype(jnp.bfloat16)
        .astype(jnp.float32)
    )


def per_device(
    tokens,
    cached_lens,
    latent_cache,
    attn_gain,
    q_weight,
    kv_down,
    latent_gain,
    kv_up,
    o_weight,
    moe_gain,
    routes,
    route_weights,
    expert_gate_up,
    expert_down,
):
    head_count = lax.axis_size("z") * lax.axis_size("core")
    swap = [(0, 1), (1, 0)]
    other_gate_up = lax.ppermute(expert_gate_up, "core", swap)
    other_down = lax.ppermute(expert_down, "core", swap)
    request = lax.axis_index("dp")
    own_rows = tokens.shape[0]
    span_len = own_rows * head_count
    length = lax.dynamic_index_in_dim(cached_lens, request, 0, keepdims=False)
    local_heads = q_weight.shape[1] // (HN + HR)
    query_width = local_heads * (HN + HR)
    normed = norm_rows(tokens.astype(jnp.float32), attn_gain).astype(jnp.bfloat16)
    shard_rows = lax.all_gather(normed, HEAD, axis=0, tiled=True)
    o_src, shard_rows = lax.optimization_barrier((o_weight, shard_rows))
    o_full = lax.all_gather(o_src, HEAD, axis=0, tiled=True)
    positions = length + jnp.arange(shard_rows.shape[0], dtype=jnp.int32)
    projected = jnp.concatenate(
        [
            query_rows(shard_rows, q_weight, positions),
            fresh_rows(shard_rows, kv_down, latent_gain, positions),
        ],
        axis=1,
    )
    queries = projected[:, :query_width]
    fresh_keys = projected[:, query_width:]
    core = lax.axis_index("core")
    quarter = latent_cache.shape[1] // 2
    mine = lax.all_to_all(
        lax.dynamic_slice_in_dim(latent_cache, core * quarter, quarter, 1),
        "dp",
        split_axis=0,
        concat_axis=1,
        tiled=True,
    )[0]
    theirs = lax.ppermute(mine, "core", swap)
    cache_rows = jnp.arange(mine.shape[0], dtype=jnp.int32)
    cache_pos = cache_rows // quarter * (2 * quarter) + cache_rows % quarter
    key_rows = jnp.concatenate([mine, theirs, fresh_keys], axis=0)
    key_wide = expand_rows(key_rows, kv_up)
    rope_keys = key_rows[:, LAT:]
    key_index = jnp.concatenate(
        [
            cache_pos + core * quarter,
            cache_pos + (1 - core) * quarter,
            CACHE + jnp.arange(span_len, dtype=jnp.int32),
        ]
    )
    block_len = min(512, span_len)

    def one_block(offset):
        block_q = lax.dynamic_slice_in_dim(queries, offset, block_len, 0)
        query_index = offset + jnp.arange(block_len, dtype=jnp.int32)
        visible = jnp.where(
            key_index[None, :] < CACHE,
            key_index[None, :] < length,
            key_index[None, :] - CACHE <= query_index[:, None],
        )
        return attend(block_q, key_wide, rope_keys, visible, local_heads)

    heads_out = lax.map(one_block, jnp.arange(0, span_len, block_len, dtype=jnp.int32)).reshape(
        span_len, local_heads * HV
    )
    heads_mine = lax.all_to_all(heads_out, HEAD, split_axis=0, concat_axis=1, tiled=True)
    group_terms = jnp.einsum(
        "tgc,gcd->gtd",
        heads_mine.reshape(own_rows, head_count, -1),
        o_full.reshape(head_count, -1, D),
        preferred_element_type=jnp.float32,
    )
    attn_out = jnp.sum(group_terms.astype(jnp.bfloat16).astype(jnp.float32), axis=0)
    hidden = tokens.astype(jnp.float32) + attn_out
    moe_in = norm_rows(hidden, moe_gain).astype(jnp.bfloat16)
    flat_routes = routes.reshape(-1)
    onehot = (flat_routes[:, None] == jnp.arange(EXPERTS, dtype=jnp.int32)[None, :]).astype(
        jnp.int32
    )
    rank_ids = jnp.sum((jnp.cumsum(onehot, axis=0) - onehot) * onehot, axis=1)
    slot_tk = (flat_routes * CAP + rank_ids).reshape(own_rows, TOPK)
    slot_iota = jnp.arange(EXPERTS * CAP, dtype=jnp.int32)
    dispatch = jnp.any(slot_tk[None, :, :] == slot_iota[:, None, None], axis=2).astype(
        jnp.bfloat16
    )
    outgoing = jnp.dot(dispatch, moe_in, preferred_element_type=jnp.float32).astype(jnp.bfloat16)
    arrived = lax.all_to_all(
        outgoing.reshape(EXPERTS, CAP, D), ("dp", "z"), split_axis=0, concat_axis=0, tiled=True
    ).reshape(EXPERTS * CAP, D)
    total = expert_half(arrived, expert_gate_up[0], expert_down[0]) + expert_half(
        arrived, other_gate_up[0], other_down[0]
    )
    returned = lax.all_to_all(
        total.astype(jnp.bfloat16).reshape(EXPERTS, CAP, D),
        ("dp", "z"),
        split_axis=0,
        concat_axis=0,
        tiled=True,
    ).reshape(EXPERTS * CAP, D)
    routed_out = jnp.zeros((own_rows, D), jnp.float32)
    for k in range(TOPK):
        pick = (slot_tk[:, k : k + 1] == slot_iota[None, :]).astype(jnp.bfloat16)
        chosen = jnp.dot(pick, returned, preferred_element_type=jnp.float32)
        routed_out = routed_out + route_weights[:, k : k + 1] * chosen
    return (hidden + routed_out).astype(jnp.bfloat16)


def solution(mesh):
    chips = jax.sharding.Mesh(
        mesh.devices.reshape(mesh.shape["dp"], -1, 2), ("dp", "z", "core")
    )
    placed = (
        P(ROWS, None),
        P(),
        P(None, "dp", None),
        P(),
        P(None, HEAD),
        P(),
        P(),
        P(None, HEAD),
        P(HEAD, None),
        P(),
        P(ROWS, None),
        P(ROWS, None),
        P(ROWS, None, None),
        P(ROWS, None, None),
    )
    return jax.shard_map(
        per_device, mesh=chips, in_specs=placed, out_specs=P(ROWS, None), check_vma=False
    )
```

profile of v0, /device:TPU:101, one launch (start us, length us, event | category | flops | bytes accessed | tf_op | source)
XLA Modules:
  0.0 352.7 jit_solution(11704750575151437512)
XLA Ops:
  6.5 1.4 fusion.38
  7.9 2.1 fusion.40
  10.0 2.2 constant_dynamic-slice_fusion.1
  12.2 3.8 %copy.92 = bf16[16,64,576]{2,1,0:T(8,128)(2,1)} copy(bf16[16,64,576]{1,2,0:T(8,128)(2,1)} %constant_dynamic-slice_fusion.1) | data formatting | bytes 2359296
  16.1 6.9 %all-to-all-start = ((bf16[16,64,576]{2,1,0:T(8,128)(2,1)}), bf16[16,64,576]{2,1,0:T(8,128)(2,1)S(1)}, u32[]{:S(2)}, u32[]{:S(2)}) async-start(bf16[16,64,576]{2,1,0:T(8,128)(2,1)} %copy.92), calls=%async_computation | async-start | bytes 2621440 | tf_op jit(solution)/shard_map/all_to_all | solution.py:144
  24.0 1.8 reduce-window.6
  28.0 11.5 %all-to-all-done = bf16[16,64,576]{2,1,0:T(8,128)(2,1)S(1)} async-done(((bf16[16,64,576]{2,1,0:T(8,128)(2,1)}), bf16[16,64,576]{2,1,0:T(8,128)(2,1)S(1)}, u32[]{:S(2)}, u32[]{:S(2)}) %all-to-all-start) | async-done | bytes 1179680 | tf_op jit(solution)/shard_map/all_to_all | solution.py:144
  39.5 1.1 copy-done.4
  40.6 1.6 copy.80
  42.2 3.1 collective-permute-start
  45.3 5.3 %fusion.71 = f32[1024,576]{0,1:T(8,128)S(1)} fusion(bf16[1024,2048]{1,0:T(8,128)(2,1)} %all-gather.3.cloned.1.call-done, bf16[2048,576]{0,1:T(8,128)(2,1)} %param.23), kind=kOutput, calls=%fused_computation.139 | convolution fusion | flops 2415919104 | bytes 8912896 | tf_op jit(solution)/shard_map/dot_general | solution.py:57
  50.8 1.3 subtract_convert_fusion.1
  52.4 11.1 %maximum_maximum_fusion = bf16[3072,576]{0,1:T(8,128)(2,1)S(1)} fusion(bf16[1024,32]{0,1:T(8,128)(2,1)S(1)} %get-tuple-element.172, bf16[1024,32]{0,1:T(8,128)(2,1)S(1)} %get-tuple-element.171, bf16[1024,512]{0,1:T(8,128)(2,1)S(1)} %multiply_convert_fusion, bf16[1024,576]{0,1:T(8,128)(2,1)S(1)} %collective-permute-done, bf16[1024,576]{0,1:T(8,128)(2,1)S(1)} %copy.80), kind=kLoop, calls=%fused_computation.30 | loop fusion | flops 17694720 | bytes 7077888 | tf_op jit(solution)/shard_map/concatenate | solution.py:154
  63.5 3.6 %convolution_convert_fusion = bf16[3072,512]{1,0:T(8,128)(2,1)} fusion(bf16[512,512]{1,0:T(8,128)(2,1)S(1)} %copy-done.24, bf16[3072,576]{0,1:T(8,128)(2,1)S(1)} %maximum_maximum_fusion), kind=kOutput, calls=%fused_computation.28 | convolution fusion | flops 1612185600 | bytes 6815744 | tf_op jit(solution)/shard_map/dot_general | solution.py:64
  67.1 4.7 %copy.81 = bf16[3072,512]{0,1:T(8,128)(2,1)} copy(bf16[3072,512]{1,0:T(8,128)(2,1)} %convolution_convert_fusion) | data formatting | bytes 6291456 | tf_op jit(solution)/shard_map/while | solution.py:176
  71.8 4.7 %fusion.70 = f32[1024,384]{0,1:T(8,128)S(1)} fusion(bf16[1024,2048]{1,0:T(8,128)(2,1)} %all-gather.3.cloned.1.call-done, bf16[2048,384]{1,0:T(8,128)(2,1)} %param.22), kind=kOutput, calls=%fused_computation.138 | convolution fusion | flops 1610612736 | bytes 7340032 | tf_op jit(solution)/shard_map/dot_general | solution.py:48
  76.7 1.0 copy-done.6
  77.8 66.5 %while.12 = (s32[]{:T(128)}, bf16[2,512,2,128]{3,2,1,0:T(2,128)(2,1)}, s32[3072]{0:T(1024)S(1)}, s32[]{:T(128)}, s32[2]{0:T(128)S(1)}, /*index=5*/bf16[1024,384]...) while((s32[]{:T(128)}, ...), condition=%wide.region_5.6_spmd, body=%wide.region_2.5_spmd.sunk | while | flops 2041721344 | bytes 64823520 | solution.py:176
  80.8 7.8 %fusion.100 = f32[2,512,3072]{2,1,0:T(8,128)} fusion(bf16[3072,2,256]{0,2,1:T(8,128)(2,1)} %bitcast.115, bf16[512,2,192]{0,2,1:T(8,128)(2,1)S(1)} %bitcast.118), kind=kOutput, calls=%fused_computation.9.clone.1 | convolution fusion | flops 805306368 | bytes 14417920 | tf_op jit(solution)/shard_map/while/body/eval_jaxpr/qhd,khd->hqk/dot_general | solution.py:72
  89.9 1.1 compare_select_fusion.2
  91.0 12.2 %fusion.101 = (f32[2,512]{1,0:T(2,128)S(1)}, f32[2,512,3072]{2,1,0:T(8,128)}) fusion(pred[512,3072]{1,0:T(8,128)(4,1)S(1)} %compare_select_fusion.2, f32[2,512,3072]{2,1,0:T(8,128)} %fusion.100, bf16[3072,64]{0,1:T(8,128)(2,1)S(1)} %get-tuple-element.277, bf16[512,2,192]{0,2,1:T(8,128)(2,1)S(1)} %bitcast.119), kind=kOutput, calls=%fused_computation.137.clone.1 | convolution fusion | flops 421530624 | bytes 28839936 | tf_op jit(solution)/shard_map/while/body/eval_jaxpr/sub | solution.py:84
  103.2 6.9 %fusion.102 = bf16[1,512,2,128]{3,1,2,0:T(8,128)(2,1)S(1)} fusion(bf16[3072,2,256]{0,2,1:T(8,128)(2,1)} %bitcast.116, f32[2,512,3072]{2,1,0:T(8,128)} %get-tuple-element.246, f32[2,512]{1,0:T(2,128)S(1)} %get-tuple-element.247), kind=kOutput, calls=%fused_computation.12.clone.1 | convolution fusion | flops 811728896 | bytes 14422016 | tf_op jit(solution)/shard_map/while/body/eval_jaxpr/hqk,khd->qhd/dot_general | solution.py:86
  110.4 0.8 copy-done.12
  114.0 7.8 %fusion.100 = f32[2,512,3072]{2,1,0:T(8,128)} fusion(bf16[3072,2,256]{0,2,1:T(8,128)(2,1)} %bitcast.115, bf16[512,2,192]{0,2,1:T(8,128)(2,1)S(1)} %bitcast.118), kind=kOutput, calls=%fused_computation.9.clone.1 | convolution fusion | flops 805306368 | bytes 14417920 | tf_op jit(solution)/shard_map/while/body/eval_jaxpr/qhd,khd->hqk/dot_general | solution.py:72
  123.0 1.1 compare_select_fusion.2
  124.2 12.1 %fusion.101 = (f32[2,512]{1,0:T(2,128)S(1)}, f32[2,512,3072]{2,1,0:T(8,128)}) fusion(pred[512,3072]{1,0:T(8,128)(4,1)S(1)} %compare_select_fusion.2, f32[2,512,3072]{2,1,0:T(8,128)} %fusion.100, bf16[3072,64]{0,1:T(8,128)(2,1)S(1)} %get-tuple-element.277, bf16[512,2,192]{0,2,1:T(8,128)(2,1)S(1)} %bitcast.119), kind=kOutput, calls=%fused_computation.137.clone.1 | convolution fusion | flops 421530624 | bytes 28839936 | tf_op jit(solution)/shard_map/while/body/eval_jaxpr/sub | solution.py:84
  136.3 6.9 %fusion.102 = bf16[1,512,2,128]{3,1,2,0:T(8,128)(2,1)S(1)} fusion(bf16[3072,2,256]{0,2,1:T(8,128)(2,1)} %bitcast.116, f32[2,512,3072]{2,1,0:T(8,128)} %get-tuple-element.246, f32[2,512]{1,0:T(2,128)S(1)} %get-tuple-element.247), kind=kOutput, calls=%fused_computation.12.clone.1 | convolution fusion | flops 811728896 | bytes 14422016 | tf_op jit(solution)/shard_map/while/body/eval_jaxpr/hqk,khd->qhd/dot_general | solution.py:86
  143.5 0.8 copy-done.12
  144.3 2.2 all_to_all.26
  146.5 4.2 %all-to-all-start.1 = ((bf16[8,128,256]{2,1,0:T(8,128)(2,1)}), bf16[8,128,256]{2,1,0:T(8,128)(2,1)S(1)}, u32[]{:S(2)}, u32[]{:S(2)}) async-start(bf16[8,128,256]{2,1,0:T(8,128)(2,1)} %all_to_all.26), calls=%async_computation.1 | async-start | bytes 1048576 | tf_op jit(solution)/shard_map/all_to_all | solution.py:179
  151.6 6.8 %all-to-all-done.1 = bf16[8,128,256]{2,1,0:T(8,128)(2,1)S(1)} async-done(((bf16[8,128,256]{2,1,0:T(8,128)(2,1)}), bf16[8,128,256]{2,1,0:T(8,128)(2,1)S(1)}, u32[]{:S(2)}, u32[]{:S(2)}) %all-to-all-start.1) | async-done | bytes 524320 | tf_op jit(solution)/shard_map/all_to_all | solution.py:179
  158.4 4.7 %convert_reduce_fusion = f32[128,2048]{1,0:T(8,128)S(1)} fusion(bf16[8,256,2048]{2,1,0:T(8,128)(2,1)} %bitcast.120, bf16[8,128,256]{2,1,0:T(8,128)(2,1)S(1)} %all-to-all-done.1), kind=kOutput, calls=%fused_computation.23 | convolution fusion | flops 1079771136 | bytes 9961472 | tf_op jit(solution)/shard_map/tgc,gcd->gtd/dot_general | solution.py:180
  163.4 3.4 convolution_convert_fusion.1
  166.8 9.1 %all-to-all-start.2 = ((bf16[64,16,2048]{2,1,0:T(8,128)(2,1)}), bf16[64,16,2048]{2,1,0:T(8,128)(2,1)}, u32[]{:S(2)}, u32[]{:S(2)}) async-start(bf16[64,16,2048]{2,1,0:T(8,128)(2,1)} %bitcast.117), calls=%async_computation.2 | async-start | bytes 8388608 | tf_op jit(solution)/shard_map/all_to_all | solution.py:200
  176.0 1.3 collective-permute-start.1
  177.4 53.7 %all-to-all-done.2 = bf16[64,16,2048]{2,1,0:T(8,128)(2,1)} async-done(((bf16[64,16,2048]{2,1,0:T(8,128)(2,1)}), bf16[64,16,2048]{2,1,0:T(8,128)(2,1)}, u32[]{:S(2)}, u32[]{:S(2)}) %all-to-all-start.2) | async-done | bytes 4194336 | tf_op jit(solution)/shard_map/all_to_all | solution.py:200
  231.1 11.0 %fusion.18 = f32[1024,1408]{1,0:T(8,128)S(1)} fusion(bf16[1024,2048]{1,0:T(8,128)(2,1)} %bitcast.17, bf16[1,2048,1408]{2,1,0:T(8,128)(2,1)} %param.30), kind=kOutput, calls=%fused_computation.26 | convolution fusion | flops 5905580032 | bytes 15728640 | tf_op jit(solution)/shard_map/dot_general | solution.py:93
  242.1 3.9 %fusion.25 = bf16[1024,2048]{1,0:T(8,128)(2,1)S(1)} fusion(bf16[1,704,2048]{2,1,0:T(8,128)(2,1)S(1)} %copy-done.23, f32[1024,1408]{1,0:T(8,128)S(1)} %fusion.18), kind=kOutput, calls=%fused_computation.39 | convolution fusion | flops 2957115392 | bytes 13369344 | tf_op jit(solution)/shard_map/dot_general | solution.py:96
  246.0 10.4 %fusion.16 = f32[1024,1408]{1,0:T(8,128)S(1)} fusion(bf16[1024,2048]{1,0:T(8,128)(2,1)} %bitcast.17, bf16[1,2048,1408]{2,1,0:T(8,128)(2,1)} %collective-permute-done.1), kind=kOutput, calls=%fused_computation.24 | convolution fusion | flops 5905580032 | bytes 15728640 | tf_op jit(solution)/shard_map/dot_general | solution.py:93
  256.5 7.1 %add_convert_fusion = bf16[1024,2048]{1,0:T(8,128)(2,1)} fusion(bf16[1024,2048]{1,0:T(8,128)(2,1)S(1)} %fusion.25, bf16[1,704,2048]{2,1,0:T(8,128)(2,1)} %collective-permute-done.2, f32[1024,1408]{1,0:T(8,128)S(1)} %fusion.16), kind=kOutput, calls=%fused_computation.22 | convolution fusion | flops 2967601152 | bytes 17563648 | tf_op jit(solution)/shard_map/dot_general | solution.py:96
  263.6 8.4 %all-to-all-start.3 = ((bf16[64,16,2048]{2,1,0:T(8,128)(2,1)}), bf16[64,16,2048]{2,1,0:T(8,128)(2,1)}, u32[]{:S(2)}, u32[]{:S(2)}) async-start(bf16[64,16,2048]{2,1,0:T(8,128)(2,1)} %bitcast.123), calls=%async_computation.3 | async-start | bytes 8388608 | tf_op jit(solution)/shard_map/all_to_all | solution.py:206
  272.1 54.5 %all-to-all-done.3 = bf16[64,16,2048]{2,1,0:T(8,128)(2,1)} async-done(((bf16[64,16,2048]{2,1,0:T(8,128)(2,1)}), bf16[64,16,2048]{2,1,0:T(8,128)(2,1)}, u32[]{:S(2)}, u32[]{:S(2)}) %all-to-all-start.3) | async-done | bytes 4194336 | tf_op jit(solution)/shard_map/all_to_all | solution.py:206
  326.6 3.0 convolution_multiply_fusion.5
  329.5 3.0 fusion.32
  332.5 3.0 fusion.31
  335.5 3.0 fusion.30
  338.5 3.2 fusion.29
  341.7 4.0 %fusion.33 = bf16[128,2048]{1,0:T(8,128)(2,1)} fusion(f32[128,2048]{1,0:T(8,128)S(1)} %fusion.29, bf16[1024,2048]{1,0:T(8,128)(2,1)} %bitcast.23, f32[128]{0:T(128)S(1)} %get-tuple-element.183, f32[128,2048]{1,0:T(8,128)S(1)} %convert_reduce_fusion, bf16[128,2048]{1,0:T(8,128)(2,1)S(1)} %copy-done.3, s32[128]{0:T(128)S(1)} %get-tuple-element.177), kind=kOutput, calls=%fused_computation.53 | convolution fusion | flops 538574848 | bytes 7341056 | tf_op jit(solution)/shard_map/dot_general | solution.py:216
  (104 shorter events, 10.0 us)
Async XLA Ops:
  6.5 3.5 copy-start
  6.5 38.7 %all-gather.3.cloned.1.call-start = ((), (), s32[]{:S(2)}) async-start(), calls=%async_computation.4 | async-start | bytes 4718592 | tf_op jit(solution)/shard_map/all_gather | solution.py:129
  12.2 10.8 %copy-start.15 = (s32[128,6]{0,1:T(8,128)S(1)}, s32[128,6]{0,1:T(8,128)}, u32[]{:S(2)}) copy-start(s32[128,6]{0,1:T(8,128)} %param.28) | copy-start | bytes 9220
  12.2 14.5 %copy-start.25 = (s32[16]{0:T(128)S(1)}, s32[16]{0:T(128)}, u32[]{:S(2)}) copy-start(s32[16]{0:T(128)} %param.19) | copy-start | bytes 196
  16.1 23.4 %all-to-all-start = ((bf16[16,64,576]{2,1,0:T(8,128)(2,1)}), bf16[16,64,576]{2,1,0:T(8,128)(2,1)S(1)}, u32[]{:S(2)}, u32[]{:S(2)}) async-start(bf16[16,64,576]{2,1,0:T(8,128)(2,1)} %copy.92), calls=%async_computation | async-start | bytes 2621440 | tf_op jit(solution)/shard_map/all_to_all | solution.py:144
  23.0 135.4 %all-gather.5.cloned.1.call-start = ((), (), s32[]{:S(2)}) async-start(), calls=%async_computation.5 | async-start | bytes 9437184 | tf_op jit(solution)/shard_map/all_gather | solution.py:131
  25.8 24.8 %copy-start.7 = (s32[64,6,128]{2,0,1:T(8,128)}, s32[64,6,128]{2,0,1:T(8,128)S(1)}, u32[]{:S(2)}) copy-start(s32[64,6,128]{2,0,1:T(8,128)S(1)} %reduce-window.6) | copy-start | bytes 589828
  39.5 1.1 copy-start.4
  42.2 10.2 %collective-permute-start = (bf16[1024,576]{0,1:T(8,128)(2,1)S(1)}, bf16[1024,576]{0,1:T(8,128)(2,1)S(1)}, u32[]{:S(2)}, u32[]{:S(2)}) collective-permute-start(bf16[1024,576]{0,1:T(8,128)(2,1)S(1)} %copy.80), channel_id=1, source_target_pairs={{0,1},{1,0},{2,3},{3,2},{4,5},{5,4},{6,7},{7,6},{8,9},{9,8},{10,11... | collective-permute-start | bytes 3538952 | tf_op jit(solution)/shard_map/ppermute | solution.py:151
  45.2 5.6 %copy-start.22 = (f32[32]{0:T(128)S(1)}, f32[32]{0:T(128)}, u32[]{:S(2)}) copy-start(f32[32]{0:T(128)} %constant.132.clone) | copy-start | bytes 388
  45.3 6.9 %copy-start.21 = (f32[512]{0:T(512)S(1)}, f32[512]{0:T(512)}, u32[]{:S(2)}) copy-start(f32[512]{0:T(512)} %param.24) | copy-start | bytes 6148
  52.1 11.4 %copy-start.9 = (bf16[1024,32]{0,1:T(8,128)(2,1)}, bf16[1024,32]{0,1:T(8,128)(2,1)S(1)}, u32[]{:S(2)}) copy-start(bf16[1024,32]{0,1:T(8,128)(2,1)S(1)} %get-tuple-element.172) | copy-start | bytes 196612
  52.3 11.1 %copy-start.24 = (bf16[512,512]{1,0:T(8,128)(2,1)S(1)}, bf16[512,512]{1,0:T(8,128)(2,1)}, u32[]{:S(2)}) copy-start(bf16[512,512]{1,0:T(8,128)(2,1)} %param.25) | copy-start | bytes 1572868
  52.4 14.7 %copy-start.5 = (bf16[1024,576]{0,1:T(8,128)(2,1)}, bf16[1024,576]{0,1:T(8,128)(2,1)S(1)}, u32[]{:S(2)}) copy-start(bf16[1024,576]{0,1:T(8,128)(2,1)S(1)} %collective-permute-done) | copy-start | bytes 3538948
  71.7 4.8 %copy-start.13 = (f32[1024,32]{0,1:T(8,128)S(1)}, f32[1024,32]{0,1:T(8,128)}, u32[]{:S(2)}) copy-start(f32[1024,32]{0,1:T(8,128)} %get-tuple-element.175) | copy-start | bytes 393220
  71.7 4.8 %copy-start.14 = (f32[1024,32]{0,1:T(8,128)S(1)}, f32[1024,32]{0,1:T(8,128)}, u32[]{:S(2)}) copy-start(f32[1024,32]{0,1:T(8,128)} %get-tuple-element.176) | copy-start | bytes 393220
  71.8 5.0 %copy-start.10 = (bf16[1024,32]{0,1:T(8,128)(2,1)S(1)}, bf16[1024,32]{0,1:T(8,128)(2,1)}, u32[]{:S(2)}) copy-start(bf16[1024,32]{0,1:T(8,128)(2,1)} %copy-done.9) | copy-start | bytes 196612
  76.5 1.3 copy-start.6
  77.8 72.9 %copy-start.8 = (s32[64,6,128]{2,0,1:T(8,128)S(1)}, s32[64,6,128]{2,0,1:T(8,128)}, u32[]{:S(2)}) copy-start(s32[64,6,128]{2,0,1:T(8,128)} %copy-done.7) | copy-start | bytes 589828
  77.8 72.9 %copy-start.17 = (s32[768]{0:T(1024)S(1)}, s32[768]{0:T(1024)}, u32[]{:S(2)}) copy-start(s32[768]{0:T(1024)} %eq.130) | copy-start | bytes 9220
  77.8 72.9 %copy-start.18 = (s32[64,7]{0,1:T(8,128)S(1)}, s32[64,7]{0,1:T(8,128)}, u32[]{:S(2)}) copy-start(s32[64,7]{0,1:T(8,128)} %reduce-window.9) | copy-start | bytes 5380
  77.8 73.3 %copy-start.16 = (s32[128,6]{0,1:T(8,128)S(1)}, s32[128,6]{0,1:T(8,128)}, u32[]{:S(2)}) copy-start(s32[128,6]{0,1:T(8,128)} %param.28) | copy-start | bytes 9220
  103.2 6.9 %copy-start.11 = (bf16[2,512,2,128]{3,2,1,0:T(2,128)(2,1)S(1)}, bf16[2,512,2,128]{3,2,1,0:T(2,128)(2,1)}, u32[]{:S(2)}) copy-start(bf16[2,512,2,128]{3,2,1,0:T(2,128)(2,1)} %get-tuple-element.260) | copy-start | bytes 1572868 | tf_op jit(solution)/shard_map/while
  110.4 0.8 copy-start.12
  136.3 6.9 %copy-start.11 = (bf16[2,512,2,128]{3,2,1,0:T(2,128)(2,1)S(1)}, bf16[2,512,2,128]{3,2,1,0:T(2,128)(2,1)}, u32[]{:S(2)}) copy-start(bf16[2,512,2,128]{3,2,1,0:T(2,128)(2,1)} %get-tuple-element.260) | copy-start | bytes 1572868 | tf_op jit(solution)/shard_map/while
  143.5 0.8 copy-start.12
  146.5 11.9 %all-to-all-start.1 = ((bf16[8,128,256]{2,1,0:T(8,128)(2,1)}), bf16[8,128,256]{2,1,0:T(8,128)(2,1)S(1)}, u32[]{:S(2)}, u32[]{:S(2)}) async-start(bf16[8,128,256]{2,1,0:T(8,128)(2,1)} %all_to_all.26), calls=%async_computation.1 | async-start | bytes 1048576 | tf_op jit(solution)/shard_map/all_to_all | solution.py:179
  158.4 4.8 %copy-start.2 = (bf16[128,2048]{1,0:T(8,128)(2,1)S(1)}, bf16[128,2048]{1,0:T(8,128)(2,1)}, u32[]{:S(2)}) copy-start(bf16[128,2048]{1,0:T(8,128)(2,1)} %param.18) | copy-start | bytes 1572868
  158.4 5.0 %copy-start.19 = (f32[2048]{0:T(1024)S(1)}, f32[2048]{0:T(1024)}, u32[]{:S(2)}) copy-start(f32[2048]{0:T(1024)} %param.27) | copy-start | bytes 24580
  166.8 64.2 %all-to-all-start.2 = ((bf16[64,16,2048]{2,1,0:T(8,128)(2,1)}), bf16[64,16,2048]{2,1,0:T(8,128)(2,1)}, u32[]{:S(2)}, u32[]{:S(2)}) async-start(bf16[64,16,2048]{2,1,0:T(8,128)(2,1)} %bitcast.117), calls=%async_computation.2 | async-start | bytes 8388608 | tf_op jit(solution)/shard_map/all_to_all | solution.py:200
  176.0 70.0 %collective-permute-start.1 = (bf16[1,2048,1408]{2,1,0:T(8,128)(2,1)}, bf16[1,2048,1408]{2,1,0:T(8,128)(2,1)}, u32[]{:S(2)}, u32[]{:S(2)}) collective-permute-start(bf16[1,2048,1408]{2,1,0:T(8,128)(2,1)} %param.30), channel_id=1, source_target_pairs={{0,1},{1,0},{2,3},{3,2},{4,5},{5,4},{6,7},{7,6},{8,9},{9,8},{10,11... | collective-permute-start | bytes 17301512 | tf_op jit(solution)/shard_map/ppermute | solution.py:120
  177.3 79.2 %collective-permute-start.2 = (bf16[1,704,2048]{2,1,0:T(8,128)(2,1)}, bf16[1,704,2048]{2,1,0:T(8,128)(2,1)}, u32[]{:S(2)}, u32[]{:S(2)}) collective-permute-start(bf16[1,704,2048]{2,1,0:T(8,128)(2,1)} %param.31), channel_id=1, source_target_pairs={{0,1},{1,0},{2,3},{3,2},{4,5},{5,4},{6,7},{7,6},{8,9},{9,8},{10,11... | collective-permute-start | bytes 8650760 | tf_op jit(solution)/shard_map/ppermute | solution.py:121
  231.1 11.0 %copy-start.23 = (bf16[1,704,2048]{2,1,0:T(8,128)(2,1)S(1)}, bf16[1,704,2048]{2,1,0:T(8,128)(2,1)}, u32[]{:S(2)}) copy-start(bf16[1,704,2048]{2,1,0:T(8,128)(2,1)} %param.31) | copy-start | bytes 8650756
  263.6 8.5 %copy-start.20 = (f32[128,6]{0,1:T(8,128)S(1)}, f32[128,6]{0,1:T(8,128)}, u32[]{:S(2)}) copy-start(f32[128,6]{0,1:T(8,128)} %param.29) | copy-start | bytes 9220
  263.6 63.0 %all-to-all-start.3 = ((bf16[64,16,2048]{2,1,0:T(8,128)(2,1)}), bf16[64,16,2048]{2,1,0:T(8,128)(2,1)}, u32[]{:S(2)}, u32[]{:S(2)}) async-start(bf16[64,16,2048]{2,1,0:T(8,128)(2,1)} %bitcast.123), calls=%async_computation.3 | async-start | bytes 8388608 | tf_op jit(solution)/shard_map/all_to_all | solution.py:206
  338.5 3.2 copy-start.3
  338.5 7.2 %copy-start.1 = (bf16[16,128,576]{1,2,0:T(8,128)(2,1)S(1)}, bf16[16,128,576]{1,2,0:T(8,128)(2,1)}, u32[]{:S(2)}) copy-start(bf16[16,128,576]{1,2,0:T(8,128)(2,1)} %param.20) | copy-start | bytes 7077892
Sparse Core Ops, SparseCore 0:
  10.2 31.7 all-gather.2
  45.4 47.9 all-gather.4
where the time goes:
time: 358 us; the launch traced here: 353 us
  matrix products  127 us (35%)
  waiting for transfers between devices  126 us (35%)
  starting transfers between devices  33.2 us (9%)
  other arithmetic  25.2 us (7%)
  local copies, waits for them, and re-layouts  22.7 us (6%)
  between operations  14.1 us (4%)
  loops' own time  4.1 us (1%)
    all_to_all x1, waiting for transfers between devices, per_device(): lax.all_to_all(total.astype(jnp.bfloat16).reshape(EXPERTS, CAP, D), ('dp'...  54.5 us
    all_to_all x1, waiting for transfers between devices, per_device(): lax.all_to_all(outgoing.reshape(EXPERTS, CAP, D), ('dp', 'z'), split_axis...  53.7 us
    sub x2, matrix products, attend(): weights = jnp.where(visible[None], jnp.exp(scores - row_max), 0.0)  24.3 us
    dot_general x2, matrix products, expert_half(): mixed_rows = jnp.dot(rows, gate_up, preferred_element_type=jnp.float32)  21.4 us
    dot_general x6, matrix products, per_device(): chosen = jnp.dot(pick, returned, preferred_element_type=jnp.float32)  19.1 us
    dot_general x2, matrix products, attend(): jnp.einsum('qhd,khd->hqk', query_heads[:, :, :HN], key_heads[:, :, :HN],...  15.6 us
    dot_general x2, matrix products, attend(): jnp.einsum('hqk,khd->qhd', prob_rows, key_heads[:, :, HN:], preferred_ele...  13.8 us
    all_to_all x1, waiting for transfers between devices, per_device(): lax.all_to_all(lax.dynamic_slice_in_dim(latent_cache, core * quarter, qua...  11.5 us
  transfers between devices with their start and end apart: 9, of which 4 were waited for; matrix products, arithmetic and copies ran while one was open for 37% of the time, Pallas kernels for 0%

commit v1 on v0

--- a/solution.py
+++ b/solution.py
@@ -2,6 +2,8 @@
 import jax.numpy as jnp
 import numpy as np
 from jax import lax
+from jax.experimental import pallas as pl
+from jax.experimental.pallas import tpu as pltpu
 from jax.sharding import PartitionSpec as P
 
 D = 2048
@@ -87,6 +89,56 @@
         "hqk,khd->qhd", prob_rows, key_heads[:, :, HN:], preferred_element_type=jnp.float32
     )
     return mixed_rows.astype(jnp.bfloat16)
+
+
+Q_BLOCK = 256
+
+
+def attend_kernel(qn_ref, qr_ref, kw_ref, kr_ref, th_ref, o_ref):
+    heads = qr_ref.shape[0]
+    first = pl.program_id(0) * Q_BLOCK
+    q_idx = first + lax.broadcasted_iota(jnp.int32, (Q_BLOCK, 1), 0)
+    visible = q_idx >= th_ref[...]
+    kr = kr_ref[...]
+    contract = (((1,), (1,)), ((), ()))
+    for h in range(heads):
+        qn = qn_ref[:, h * HN : (h + 1) * HN]
+        kn = kw_ref[:, h * (HN + HV) : h * (HN + HV) + HN]
+        vals = kw_ref[:, h * (HN + HV) + HN : (h + 1) * (HN + HV)]
+        scores = lax.dot_general(qn, kn, contract, preferred_element_type=jnp.float32)
+        scores = scores + lax.dot_general(
+            qr_ref[h], kr, contract, preferred_element_type=jnp.float32
+        )
+        scores = scores * (HN + HR) ** (-0.5)
+        scores = jnp.where(visible, scores, -1e30)
+        row_max = jnp.max(scores, axis=1, keepdims=True)
+        weights = jnp.where(visible, jnp.exp(scores - row_max), 0.0)
+        prob_rows = (weights / jnp.sum(weights, axis=1, keepdims=True)).astype(jnp.bfloat16)
+        mixed = jnp.dot(prob_rows, vals, preferred_element_type=jnp.float32)
+        o_ref[:, h * HV : (h + 1) * HV] = mixed.astype(jnp.bfloat16)
+
+
+def attend_all(q_nope, q_rope, key_wide, rope_keys, thresh, interpret=False):
+    span, nope_width = q_nope.shape
+    heads = q_rope.shape[0]
+    keys = key_wide.shape[0]
+    return pl.pallas_call(
+        attend_kernel,
+        grid=(span // Q_BLOCK,),
+        in_specs=[
+            pl.BlockSpec((Q_BLOCK, nope_width), lambda i: (i, 0)),
+            pl.BlockSpec((heads, Q_BLOCK, HR), lambda i: (0, i, 0)),
+            pl.BlockSpec((keys, key_wide.shape[1]), lambda i: (0, 0)),
+            pl.BlockSpec((keys, HR), lambda i: (0, 0)),
+            pl.BlockSpec((1, keys), lambda i: (0, 0)),
+        ],
+        out_specs=pl.BlockSpec((Q_BLOCK, heads * HV), lambda i: (i, 0)),
+        out_shape=jax.ShapeDtypeStruct((span, heads * HV), jnp.bfloat16),
+        compiler_params=pltpu.CompilerParams(
+            dimension_semantics=("arbitrary",), vmem_limit_bytes=48 * 1024 * 1024
+        ),
+        interpret=interpret,
+    )(q_nope, q_rope, key_wide, rope_keys, thresh)
 
 
 def expert_half(rows, gate_up, down):
@@ -161,20 +213,16 @@
             CACHE + jnp.arange(span_len, dtype=jnp.int32),
         ]
     )
-    block_len = min(512, span_len)
-
-    def one_block(offset):
-        block_q = lax.dynamic_slice_in_dim(queries, offset, block_len, 0)
-        query_index = offset + jnp.arange(block_len, dtype=jnp.int32)
-        visible = jnp.where(
-            key_index[None, :] < CACHE,
-            key_index[None, :] < length,
-            key_index[None, :] - CACHE <= query_index[:, None],
-        )
-        return attend(block_q, key_wide, rope_keys, visible, local_heads)
-
-    heads_out = lax.map(one_block, jnp.arange(0, span_len, block_len, dtype=jnp.int32)).reshape(
-        span_len, local_heads * HV
+    thresh = jnp.where(
+        key_index < CACHE, jnp.where(key_index < length, -1, 1 << 30), key_index - CACHE
+    ).reshape(1, -1)
+    query_heads = queries.reshape(span_len, local_heads, HN + HR)
+    heads_out = attend_all(
+        query_heads[:, :, :HN].reshape(span_len, local_heads * HN),
+        query_heads[:, :, HN:].transpose(1, 0, 2),
+        key_wide,
+        rope_keys,
+        thresh,
     )
     heads_mine = lax.all_to_all(heads_out, HEAD, split_axis=0, concat_axis=1, tiled=True)
     group_terms = jnp.einsum(

time: 358 us -> 351 us (0.980)
  matrix products: 127 us -> 71.6 us
  blocking collectives: 0 us -> 24.2 us
  waiting for transfers between devices: 126 us -> 147 us
  Pallas kernels: 0 us -> 19.2 us
  local copies, waits for them, and re-layouts: 22.7 us -> 12.3 us
  loops' own time: 4.1 us -> 0 us
    all_gather x1, waiting for transfers between devices: 0.01 us -> 31.8 us  [per_device(): shard_rows = lax.all_gather(normed, HEAD, axis=0, tiled=True)]
    dot_general x4 -> x0, matrix products: 29.3 us -> none  [the longest x2 15.6 us: attend(): jnp.einsum('qhd,khd->hqk', query_heads[:, :, :HN], key_heads[:, :, :HN],...]
    sub x2 -> x0, matrix products: 24.3 us -> none  [attend(): weights = jnp.where(visible[None], jnp.exp(scores - row_max), 0.0)]
    all_to_all x0 -> x1, blocking collectives: none -> 24.2 us  [per_device(): lax.all_to_all(lax.dynamic_slice_in_dim(latent_cache, core * quarter, qua...]
    pallas_call x0 -> x1, Pallas kernels: none -> 19.2 us  [attend_all(): pl.pallas_call(attend_kernel, grid=(span // Q_BLOCK,), in_specs=[pl.Block...]
    all_to_all x1, starting transfers between devices: 4.23 us -> 16.1 us  [per_device(): lax.all_to_all(heads_out, HEAD, split_axis=0, concat_axis=1, tiled=True)]
    all_to_all x1 -> x0, waiting for transfers between devices: 11.5 us -> none  [per_device(): lax.all_to_all(lax.dynamic_slice_in_dim(latent_cache, core * quarter, qua...]
    all_to_all x1 -> x0, starting transfers between devices: 6.89 us -> none  [per_device(): lax.all_to_all(lax.dynamic_slice_in_dim(latent_cache, core * quarter, qua...]
  transfers between devices with their start and end apart: 9 -> 8, of which waited for: 4 -> 4; matrix products, arithmetic and copies ran while one was open for 37% -> 19% of each run, Pallas kernels for 0% -> 6%
where the time goes in v1:
time: 351 us; the launch traced here: 347 us
  waiting for transfers between devices  147 us (42%)
  matrix products  71.6 us (20%)
  starting transfers between devices  36 us (10%)
  blocking collectives  24.2 us (7%)
  other arithmetic  22.5 us (6%)
  Pallas kernels  19.2 us (5%)
  between operations  14.1 us (4%)
  local copies, waits for them, and re-layouts  12.3 us (4%)
    all_to_all x1, waiting for transfers between devices, per_device(): lax.all_to_all(total.astype(jnp.bfloat16).reshape(EXPERTS, CAP, D), ('dp'...  54.5 us
    all_to_all x1, waiting for transfers between devices, per_device(): lax.all_to_all(outgoing.reshape(EXPERTS, CAP, D), ('dp', 'z'), split_axis...  53.8 us
    all_gather x1, waiting for transfers between devices, per_device(): shard_rows = lax.all_gather(normed, HEAD, axis=0, tiled=True)  31.8 us
    all_to_all x1, blocking collectives, per_device(): lax.all_to_all(lax.dynamic_slice_in_dim(latent_cache, core * quarter, qua...  24.2 us
    dot_general x2, matrix products, expert_half(): mixed_rows = jnp.dot(rows, gate_up, preferred_element_type=jnp.float32)  21 us
    pallas_call x1, Pallas kernels, attend_all(): pl.pallas_call(attend_kernel, grid=(span // Q_BLOCK,), in_specs=[pl.Block...  19.2 us
    dot_general x6, matrix products, per_device(): chosen = jnp.dot(pick, returned, preferred_element_type=jnp.float32)  19.1 us
    all_to_all x1, starting transfers between devices, per_device(): lax.all_to_all(heads_out, HEAD, split_axis=0, concat_axis=1, tiled=True)  16.1 us
  transfers between devices with their start and end apart: 8, of which 4 were waited for; matrix products, arithmetic and copies ran while one was open for 19% of the time, Pallas kernels for 6%

profile of v1, /device:TPU:101, one launch (start us, length us, event | category | flops | bytes accessed | tf_op | source)
XLA Modules:
  0.0 347.0 jit_solution(18434522894457942738)
XLA Ops:
  6.5 1.4 fusion.22
  7.9 2.0 fusion.24
  10.0 31.8 %all-gather.3.cloned.1.call-done = bf16[1024,2048]{1,0:T(8,128)(2,1)} async-done(((bf16[128,2048]{1,0:T(8,128)(2,1)}), bf16[1024,2048]{1,0:T(8,128)(2,1)}) %all-gather.3.cloned.1.call-update) | async-done | bytes 4194320 | tf_op jit(solution)/shard_map/all_gather | solution.py:181
  41.9 2.1 constant_dynamic-slice_fusion
  44.0 3.8 %copy.92 = bf16[16,64,576]{2,1,0:T(8,128)(2,1)} copy(bf16[16,64,576]{1,2,0:T(8,128)(2,1)} %constant_dynamic-slice_fusion) | data formatting | bytes 2359296
  47.9 24.2 %all_to_all.35 = bf16[16,64,576]{2,1,0:T(8,128)(2,1)S(1)} all-to-all(bf16[16,64,576]{2,1,0:T(8,128)(2,1)} %copy.92), channel_id=1, replica_groups=mesh['dp'=16,'z'=4,'core'=2] {'dp'}, dimensions={0} | all-to-all | bytes 2359296 | tf_op jit(solution)/shard_map/all_to_all | solution.py:196
  72.1 1.5 copy.79
  73.6 1.5 collective-permute-start
  75.5 1.8 reduce-window.6
  77.3 0.3 slice_reduce_fusion
  77.6 0.6 dynamic_slice.7
  78.2 0.6 add_convert_fusion.3
  78.9 0.7 compare_select_fusion.1.th_ref
  79.6 1.5 copy.83
  81.1 4.5 %fusion.50 = f32[1024,384]{0,1:T(8,128)S(1)} fusion(bf16[1024,2048]{1,0:T(8,128)(2,1)} %all-gather.3.cloned.1.call-done, bf16[2048,384]{1,0:T(8,128)(2,1)} %param.20), kind=kOutput, calls=%fused_computation.117 | convolution fusion | flops 1610612736 | bytes 7340032 | tf_op jit(solution)/shard_map/dot_general | solution.py:50
  85.7 0.3 copy.90
  86.0 0.3 copy.91
  86.6 6.0 %fusion.51 = f32[1024,576]{1,0:T(8,128)S(1)} fusion(bf16[1024,2048]{1,0:T(8,128)(2,1)} %all-gather.3.cloned.1.call-done, bf16[2048,576]{0,1:T(8,128)(2,1)} %param.21), kind=kOutput, calls=%fused_computation.118 | convolution fusion | flops 2415919104 | bytes 8912896 | tf_op jit(solution)/shard_map/dot_general | solution.py:59
  92.6 2.2 subtract_convert_fusion.1
  94.9 0.4 subtract_convert_fusion
  95.3 0.3 maximum_bitcast_fusion.qr_ref
  95.8 0.2 multiply_convert_fusion
  96.1 0.5 copy-done.3
  96.6 0.4 copy-done.6
  97.0 0.2 maximum_maximum_fusion.1.kr_ref
  97.2 11.4 %maximum_maximum_fusion = bf16[3072,576]{1,0:T(8,128)(2,1)S(1)} fusion(bf16[1024,32]{1,0:T(8,128)(2,1)S(1)} %get-tuple-element.12, bf16[1024,32]{1,0:T(8,128)(2,1)S(1)} %get-tuple-element.11, bf16[1024,512]{1,0:T(8,128)(2,1)S(1)} %multiply_convert_fusion, bf16[1024,576]{1,0:T(8,128)(2,1)S(1)} %copy-done.6, bf16[1024,576]{1,0:T(8,128)(2,1)S(1)} %bitcast.92), kind=kLoop, calls=%fused_computation.7 | loop fusion | flops 17694720 | bytes 7077888 | tf_op jit(solution)/shard_map/concatenate | solution.py:206
  108.7 1.8 convolution_convert_fusion.kw_ref
  110.5 19.2 %shard_map.154 = bf16[1024,256]{1,0:T(8,128)(2,1)} custom-call(bf16[1024,256]{1,0:T(8,128)(2,1)S(1)} %copy.84.qn_ref, bf16[2,1024,64]{2,1,0:T(8,128)(2,1)S(1)} %maximum_bitcast_fusion.qr_ref, bf16[3072,512]{1,0:T(8,128)(2,1)S(1)} %convolution_convert_fusion.kw_ref, bf16[3072,64]{1,0:T(8,128)(2,1)S(1)} %maximum_maximum_fusion.1.kr_ref, ...), custom_call_target="tpu_custom_call" | custom-call | tf_op jit(solution)/shard_map/pallas_call | solution.py:125
  129.7 16.1 %all-to-all-start.1 = ((bf16[8,128,256]{2,1,0:T(8,128)(2,1)}), bf16[8,128,256]{2,1,0:T(8,128)(2,1)S(1)}, u32[]{:S(2)}, u32[]{:S(2)}) async-start(bf16[8,128,256]{2,1,0:T(8,128)(2,1)} %bitcast.8), calls=%async_computation.1 | async-start | bytes 1048576 | tf_op jit(solution)/shard_map/all_to_all | solution.py:227
  146.1 0.5 fusion.7
  146.6 6.7 %all-to-all-done.1 = bf16[8,128,256]{2,1,0:T(8,128)(2,1)S(1)} async-done(((bf16[8,128,256]{2,1,0:T(8,128)(2,1)}), bf16[8,128,256]{2,1,0:T(8,128)(2,1)S(1)}, u32[]{:S(2)}, u32[]{:S(2)}) %all-to-all-start.1) | async-done | bytes 524320 | tf_op jit(solution)/shard_map/all_to_all | solution.py:227
  153.4 4.7 %convert_reduce_fusion = f32[128,2048]{1,0:T(8,128)S(1)} fusion(bf16[8,256,2048]{2,1,0:T(8,128)(2,1)} %bitcast.93, bf16[8,128,256]{2,1,0:T(8,128)(2,1)S(1)} %all-to-all-done.1), kind=kOutput, calls=%fused_computation.1 | convolution fusion | flops 1079771136 | bytes 9961472 | tf_op jit(solution)/shard_map/tgc,gcd->gtd/dot_general | solution.py:228
  158.4 3.4 convolution_convert_fusion.1
  161.8 8.5 %all-to-all-start.2 = ((bf16[64,16,2048]{2,1,0:T(8,128)(2,1)}), bf16[64,16,2048]{2,1,0:T(8,128)(2,1)}, u32[]{:S(2)}, u32[]{:S(2)}) async-start(bf16[64,16,2048]{2,1,0:T(8,128)(2,1)} %bitcast.89), calls=%async_computation.2 | async-start | bytes 8388608 | tf_op jit(solution)/shard_map/all_to_all | solution.py:248
  170.3 1.3 collective-permute-start.1
  171.7 53.8 %all-to-all-done.2 = bf16[64,16,2048]{2,1,0:T(8,128)(2,1)} async-done(((bf16[64,16,2048]{2,1,0:T(8,128)(2,1)}), bf16[64,16,2048]{2,1,0:T(8,128)(2,1)}, u32[]{:S(2)}, u32[]{:S(2)}) %all-to-all-start.2) | async-done | bytes 4194336 | tf_op jit(solution)/shard_map/all_to_all | solution.py:248
  225.6 10.6 %fusion.2 = f32[1024,1408]{1,0:T(8,128)S(1)} fusion(bf16[1024,2048]{1,0:T(8,128)(2,1)} %bitcast.15, bf16[1,2048,1408]{2,1,0:T(8,128)(2,1)} %param.28), kind=kOutput, calls=%fused_computation.4 | convolution fusion | flops 5905580032 | bytes 15728640 | tf_op jit(solution)/shard_map/dot_general | solution.py:145
  236.2 3.9 %fusion.9 = bf16[1024,2048]{1,0:T(8,128)(2,1)S(1)} fusion(bf16[1,704,2048]{2,1,0:T(8,128)(2,1)S(1)} %copy-done.12, f32[1024,1408]{1,0:T(8,128)S(1)} %fusion.2), kind=kOutput, calls=%fused_computation.17 | convolution fusion | flops 2957115392 | bytes 13369344 | tf_op jit(solution)/shard_map/dot_general | solution.py:148
  240.1 10.4 %fusion = f32[1024,1408]{1,0:T(8,128)S(1)} fusion(bf16[1024,2048]{1,0:T(8,128)(2,1)} %bitcast.15, bf16[1,2048,1408]{2,1,0:T(8,128)(2,1)} %collective-permute-done.1), kind=kOutput, calls=%fused_computation.2 | convolution fusion | flops 5905580032 | bytes 15728640 | tf_op jit(solution)/shard_map/dot_general | solution.py:145
  250.6 7.1 %add_convert_fusion = bf16[1024,2048]{1,0:T(8,128)(2,1)} fusion(bf16[1024,2048]{1,0:T(8,128)(2,1)S(1)} %fusion.9, bf16[1,704,2048]{2,1,0:T(8,128)(2,1)} %collective-permute-done.2, f32[1024,1408]{1,0:T(8,128)S(1)} %fusion), kind=kOutput, calls=%fused_computation | convolution fusion | flops 2967601152 | bytes 17563648 | tf_op jit(solution)/shard_map/dot_general | solution.py:148
  257.7 8.5 %all-to-all-start.3 = ((bf16[64,16,2048]{2,1,0:T(8,128)(2,1)}), bf16[64,16,2048]{2,1,0:T(8,128)(2,1)}, u32[]{:S(2)}, u32[]{:S(2)}) async-start(bf16[64,16,2048]{2,1,0:T(8,128)(2,1)} %bitcast.94), calls=%async_computation.3 | async-start | bytes 8388608 | tf_op jit(solution)/shard_map/all_to_all | solution.py:254
  266.2 54.5 %all-to-all-done.3 = bf16[64,16,2048]{2,1,0:T(8,128)(2,1)} async-done(((bf16[64,16,2048]{2,1,0:T(8,128)(2,1)}), bf16[64,16,2048]{2,1,0:T(8,128)(2,1)}, u32[]{:S(2)}, u32[]{:S(2)}) %all-to-all-start.3) | async-done | bytes 4194336 | tf_op jit(solution)/shard_map/all_to_all | solution.py:254
  320.7 3.0 convolution_multiply_fusion.5
  323.7 3.0 fusion.16
  326.7 3.0 fusion.15
  329.7 3.0 fusion.14
  332.7 3.2 fusion.13
  335.9 4.0 %fusion.17 = bf16[128,2048]{1,0:T(8,128)(2,1)} fusion(f32[128,2048]{1,0:T(8,128)S(1)} %fusion.13, bf16[1024,2048]{1,0:T(8,128)(2,1)} %bitcast.21, f32[128]{0:T(128)S(1)} %get-tuple-element.23, f32[128,2048]{1,0:T(8,128)S(1)} %convert_reduce_fusion, bf16[128,2048]{1,0:T(8,128)(2,1)S(1)} %copy-done.5, s32[128]{0:T(128)S(1)} %get-tuple-element.17), kind=kOutput, calls=%fused_computation.31 | convolution fusion | flops 538574848 | bytes 7341056 | tf_op jit(solution)/shard_map/dot_general | solution.py:264
  (59 shorter events, 1.8 us)
Async XLA Ops:
  6.5 35.4 %copy-start = (bf16[16,128,576]{1,2,0:T(8,128)(2,1)S(1)}, bf16[16,128,576]{1,2,0:T(8,128)(2,1)}, u32[]{:S(2)}) copy-start(bf16[16,128,576]{1,2,0:T(8,128)(2,1)} %param.18) | copy-start | bytes 7077892
  6.5 35.3 %all-gather.3.cloned.1.call-start = ((), (), s32[]{:S(2)}) async-start(), calls=%async_computation.4 | async-start | bytes 4718592 | tf_op jit(solution)/shard_map/all_gather | solution.py:181
  10.0 143.4 %all-gather.5.cloned.1.call-start = ((), (), s32[]{:S(2)}) async-start(), calls=%async_computation.5 | async-start | bytes 9437184 | tf_op jit(solution)/shard_map/all_gather | solution.py:183
  44.0 31.1 %copy-start.7 = (s32[128,6]{0,1:T(8,128)S(1)}, s32[128,6]{0,1:T(8,128)}, u32[]{:S(2)}) copy-start(s32[128,6]{0,1:T(8,128)} %param.26) | copy-start | bytes 9220
  47.9 29.8 %copy-start.14 = (s32[16]{0:T(128)S(1)}, s32[16]{0:T(128)}, u32[]{:S(2)}) copy-start(s32[16]{0:T(128)} %param.17) | copy-start | bytes 196
  72.1 6.8 %copy-start.2 = (bf16[16,64,576]{2,1,0:T(8,128)(2,1)}, bf16[16,64,576]{2,1,0:T(8,128)(2,1)S(1)}, u32[]{:S(2)}) copy-start(bf16[16,64,576]{2,1,0:T(8,128)(2,1)S(1)} %all_to_all.35) | copy-start | bytes 3538948
  73.6 6.0 %collective-permute-start = (bf16[1024,576]{0,1:T(8,128)(2,1)}, bf16[1024,576]{0,1:T(8,128)(2,1)S(1)}, u32[]{:S(2)}, u32[]{:S(2)}) collective-permute-start(bf16[1024,576]{0,1:T(8,128)(2,1)} %copy.79), channel_id=1, source_target_pairs={{0,1},{1,0},{2,3},{3,2},{4,5},{5,4},{6,7},{7,6},{8,9},{9,8},{10,11... | collective-permute-start | bytes 3538952 | tf_op jit(solution)/shard_map/ppermute | solution.py:203
  86.6 6.0 %copy-start.11 = (f32[32]{0:T(128)S(1)}, f32[32]{0:T(128)}, u32[]{:S(2)}) copy-start(f32[32]{0:T(128)} %constant.84.clone) | copy-start | bytes 388
  94.8 1.0 copy-start.10
  95.3 1.3 copy-start.3
  95.3 1.7 copy-start.6
  97.2 11.5 %copy-start.13 = (bf16[512,512]{1,0:T(8,128)(2,1)S(1)}, bf16[512,512]{1,0:T(8,128)(2,1)}, u32[]{:S(2)}) copy-start(bf16[512,512]{1,0:T(8,128)(2,1)} %param.23) | copy-start | bytes 1572868
  129.7 23.7 %all-to-all-start.1 = ((bf16[8,128,256]{2,1,0:T(8,128)(2,1)}), bf16[8,128,256]{2,1,0:T(8,128)(2,1)S(1)}, u32[]{:S(2)}, u32[]{:S(2)}) async-start(bf16[8,128,256]{2,1,0:T(8,128)(2,1)} %bitcast.8), calls=%async_computation.1 | async-start | bytes 1048576 | tf_op jit(solution)/shard_map/all_to_all | solution.py:227
  153.4 4.8 %copy-start.4 = (bf16[128,2048]{1,0:T(8,128)(2,1)S(1)}, bf16[128,2048]{1,0:T(8,128)(2,1)}, u32[]{:S(2)}) copy-start(bf16[128,2048]{1,0:T(8,128)(2,1)} %param.16) | copy-start | bytes 1572868
  153.4 5.0 %copy-start.8 = (f32[2048]{0:T(1024)S(1)}, f32[2048]{0:T(1024)}, u32[]{:S(2)}) copy-start(f32[2048]{0:T(1024)} %param.25) | copy-start | bytes 24580
  161.8 63.8 %all-to-all-start.2 = ((bf16[64,16,2048]{2,1,0:T(8,128)(2,1)}), bf16[64,16,2048]{2,1,0:T(8,128)(2,1)}, u32[]{:S(2)}, u32[]{:S(2)}) async-start(bf16[64,16,2048]{2,1,0:T(8,128)(2,1)} %bitcast.89), calls=%async_computation.2 | async-start | bytes 8388608 | tf_op jit(solution)/shard_map/all_to_all | solution.py:248
  170.3 69.8 %collective-permute-start.1 = (bf16[1,2048,1408]{2,1,0:T(8,128)(2,1)}, bf16[1,2048,1408]{2,1,0:T(8,128)(2,1)}, u32[]{:S(2)}, u32[]{:S(2)}) collective-permute-start(bf16[1,2048,1408]{2,1,0:T(8,128)(2,1)} %param.28), channel_id=1, source_target_pairs={{0,1},{1,0},{2,3},{3,2},{4,5},{5,4},{6,7},{7,6},{8,9},{9,8},{10,11... | collective-permute-start | bytes 17301512 | tf_op jit(solution)/shard_map/ppermute | solution.py:172
  171.6 78.9 %collective-permute-start.2 = (bf16[1,704,2048]{2,1,0:T(8,128)(2,1)}, bf16[1,704,2048]{2,1,0:T(8,128)(2,1)}, u32[]{:S(2)}, u32[]{:S(2)}) collective-permute-start(bf16[1,704,2048]{2,1,0:T(8,128)(2,1)} %param.29), channel_id=1, source_target_pairs={{0,1},{1,0},{2,3},{3,2},{4,5},{5,4},{6,7},{7,6},{8,9},{9,8},{10,11... | collective-permute-start | bytes 8650760 | tf_op jit(solution)/shard_map/ppermute | solution.py:173
  225.6 10.6 %copy-start.12 = (bf16[1,704,2048]{2,1,0:T(8,128)(2,1)S(1)}, bf16[1,704,2048]{2,1,0:T(8,128)(2,1)}, u32[]{:S(2)}) copy-start(bf16[1,704,2048]{2,1,0:T(8,128)(2,1)} %param.29) | copy-start | bytes 8650756
  257.7 8.5 %copy-start.9 = (f32[128,6]{0,1:T(8,128)S(1)}, f32[128,6]{0,1:T(8,128)}, u32[]{:S(2)}) copy-start(f32[128,6]{0,1:T(8,128)} %param.27) | copy-start | bytes 9220
  257.7 63.1 %all-to-all-start.3 = ((bf16[64,16,2048]{2,1,0:T(8,128)(2,1)}), bf16[64,16,2048]{2,1,0:T(8,128)(2,1)}, u32[]{:S(2)}, u32[]{:S(2)}) async-start(bf16[64,16,2048]{2,1,0:T(8,128)(2,1)} %bitcast.94), calls=%async_computation.3 | async-start | bytes 8388608 | tf_op jit(solution)/shard_map/all_to_all | solution.py:254
  332.7 3.2 copy-start.5
  332.7 7.2 %copy-start.1 = (bf16[16,128,576]{1,2,0:T(8,128)(2,1)S(1)}, bf16[16,128,576]{1,2,0:T(8,128)(2,1)}, u32[]{:S(2)}) copy-start(bf16[16,128,576]{1,2,0:T(8,128)(2,1)} %param.18) | copy-start | bytes 7077892
Sparse Core Ops, SparseCore 0:
  10.1 31.7 all-gather.2
  43.6 49.6 all-gather.4

commit v2 on v1

--- a/solution.py
+++ b/solution.py
@@ -94,11 +94,9 @@
 Q_BLOCK = 256
 
 
-def attend_kernel(qn_ref, qr_ref, kw_ref, kr_ref, th_ref, o_ref):
+def attend_kernel(qn_ref, qr_ref, kw_ref, kr_ref, th_ref, tq_ref, o_ref):
     heads = qr_ref.shape[0]
-    first = pl.program_id(0) * Q_BLOCK
-    q_idx = first + lax.broadcasted_iota(jnp.int32, (Q_BLOCK, 1), 0)
-    visible = q_idx >= th_ref[...]
+    visible = tq_ref[...] >= th_ref[...]
     kr = kr_ref[...]
     contract = (((1,), (1,)), ((), ()))
     for h in range(heads):
@@ -118,7 +116,7 @@
         o_ref[:, h * HV : (h + 1) * HV] = mixed.astype(jnp.bfloat16)
 
 
-def attend_all(q_nope, q_rope, key_wide, rope_keys, thresh, interpret=False):
+def attend_all(q_nope, q_rope, key_wide, rope_keys, thresh, q_tokens, interpret=False):
     span, nope_width = q_nope.shape
     heads = q_rope.shape[0]
     keys = key_wide.shape[0]
@@ -131,6 +129,7 @@
             pl.BlockSpec((keys, key_wide.shape[1]), lambda i: (0, 0)),
             pl.BlockSpec((keys, HR), lambda i: (0, 0)),
             pl.BlockSpec((1, keys), lambda i: (0, 0)),
+            pl.BlockSpec((Q_BLOCK, 1), lambda i: (i, 0)),
         ],
         out_specs=pl.BlockSpec((Q_BLOCK, heads * HV), lambda i: (i, 0)),
         out_shape=jax.ShapeDtypeStruct((span, heads * HV), jnp.bfloat16),
@@ -138,7 +137,7 @@
             dimension_semantics=("arbitrary",), vmem_limit_bytes=48 * 1024 * 1024
         ),
         interpret=interpret,
-    )(q_nope, q_rope, key_wide, rope_keys, thresh)
+    )(q_nope, q_rope, key_wide, rope_keys, thresh, q_tokens)
 
 
 def expert_half(rows, gate_up, down):
@@ -178,10 +177,19 @@
     local_heads = q_weight.shape[1] // (HN + HR)
     query_width = local_heads * (HN + HR)
     normed = norm_rows(tokens.astype(jnp.float32), attn_gain).astype(jnp.bfloat16)
-    shard_rows = lax.all_gather(normed, HEAD, axis=0, tiled=True)
+    z_count = lax.axis_size("z")
+    shard_rows = lax.all_gather(
+        lax.all_gather(normed, "z", axis=0, tiled=True), "core", axis=0, tiled=True
+    )
     o_src, shard_rows = lax.optimization_barrier((o_weight, shard_rows))
-    o_full = lax.all_gather(o_src, HEAD, axis=0, tiled=True)
-    positions = length + jnp.arange(shard_rows.shape[0], dtype=jnp.int32)
+    o_full = lax.all_gather(
+        lax.all_gather(o_src, "z", axis=0, tiled=True), "core", axis=0, tiled=True
+    )
+    row_ids = jnp.arange(span_len, dtype=jnp.int32)
+    token_of_row = (
+        (row_ids // own_rows % z_count) * (head_count // z_count) + row_ids // (own_rows * z_count)
+    ) * own_rows + row_ids % own_rows
+    positions = length + token_of_row
     projected = jnp.concatenate(
         [
             query_rows(shard_rows, q_weight, positions),
@@ -210,7 +218,7 @@
         [
             cache_pos + core * quarter,
             cache_pos + (1 - core) * quarter,
-            CACHE + jnp.arange(span_len, dtype=jnp.int32),
+            CACHE + token_of_row,
         ]
     )
     thresh = jnp.where(
@@ -223,8 +231,11 @@
         key_wide,
         rope_keys,
         thresh,
-    )
-    heads_mine = lax.all_to_all(heads_out, HEAD, split_axis=0, concat_axis=1, tiled=True)
+        token_of_row.reshape(-1, 1),
+    )
+    heads_mine = lax.all_to_all(
+        heads_out, ("core", "z"), split_axis=0, concat_axis=1, tiled=True
+    )
     group_terms = jnp.einsum(
         "tgc,gcd->gtd",
         heads_mine.reshape(own_rows, head_count, -1),
@@ -258,11 +269,15 @@
         concat_axis=0,
         tiled=True,
     ).reshape(EXPERTS * CAP, D)
-    routed_out = jnp.zeros((own_rows, D), jnp.float32)
-    for k in range(TOPK):
-        pick = (slot_tk[:, k : k + 1] == slot_iota[None, :]).astype(jnp.bfloat16)
-        chosen = jnp.dot(pick, returned, preferred_element_type=jnp.float32)
-        routed_out = routed_out + route_weights[:, k : k + 1] * chosen
+    slot_weights = jnp.sum(
+        jnp.where(slot_tk[:, :, None] == slot_iota[None, None, :], route_weights[:, :, None], 0.0),
+        axis=1,
+    )
+    weights_hi = slot_weights.astype(jnp.bfloat16)
+    weights_lo = (slot_weights - weights_hi.astype(jnp.float32)).astype(jnp.bfloat16)
+    routed_out = jnp.dot(weights_hi, returned, preferred_element_type=jnp.float32) + jnp.dot(
+        weights_lo, returned, preferred_element_type=jnp.float32
+    )
     return (hidden + routed_out).astype(jnp.bfloat16)
 
 

time: 351 us -> 412 us (1.17)
  waiting for transfers between devices: 147 us -> 229 us
  blocking collectives: 24.2 us -> 0 us
  matrix products: 71.6 us -> 59.7 us
  starting transfers between devices: 36 us -> 46.6 us
    all_gather x2 -> x4, waiting for transfers between devices: 31.8 us -> 99.4 us  [the longest x1 48.6 us: per_device(): lax.all_gather(o_src, 'z', axis=0, tiled=True)]
    all_to_all x1 -> x0, blocking collectives: 24.2 us -> none  [per_device(): lax.all_to_all(lax.dynamic_slice_in_dim(latent_cache, core * quarter, qua...]
    all_to_all x1 -> x2, waiting for transfers between devices: 6.75 us -> 22.5 us  [the longest x1 15.8 us: per_device(): lax.all_to_all(lax.dynamic_slice_in_dim(latent_cache, core * quarter, qua...]
    dot_general x6 -> x2, matrix products: 19.1 us -> 7.19 us  [the longest x1 3.98 us: per_device(): jnp.dot(weights_lo, returned, preferred_element_type=jnp.float32)]
    all_to_all x1 -> x2, starting transfers between devices: 16.1 us -> 23.7 us  [the longest x1 16.9 us: per_device(): lax.all_to_all(heads_out, ('core', 'z'), split_axis=0, concat_axis=1, til...]
  transfers between devices with their start and end apart: 8 -> 11, of which waited for: 4 -> 7; matrix products, arithmetic and copies ran while one was open for 19% -> 17% of each run, Pallas kernels for 6% -> 5%
where the time goes in v2:
time: 412 us; the launch traced here: 406 us
  waiting for transfers between devices  229 us (56%)
  matrix products  59.7 us (14%)
  starting transfers between devices  46.6 us (11%)
  other arithmetic  23.9 us (6%)
  Pallas kernels  19.3 us (5%)
  local copies, waits for them, and re-layouts  14.1 us (3%)
  between operations  13.7 us (3%)
    all_to_all x1, waiting for transfers between devices, per_device(): lax.all_to_all(outgoing.reshape(EXPERTS, CAP, D), ('dp', 'z'), split_axis...  56.3 us
    all_to_all x1, waiting for transfers between devices, per_device(): lax.all_to_all(total.astype(jnp.bfloat16).reshape(EXPERTS, CAP, D), ('dp'...  50.5 us
    all_gather x1, waiting for transfers between devices, per_device(): lax.all_gather(o_src, 'z', axis=0, tiled=True)  48.6 us
    all_gather x1, waiting for transfers between devices, per_device(): lax.all_gather(normed, 'z', axis=0, tiled=True)  30 us
    dot_general x2, matrix products, expert_half(): mixed_rows = jnp.dot(rows, gate_up, preferred_element_type=jnp.float32)  21 us
    all_gather x1, waiting for transfers between devices, per_device(): lax.all_gather(lax.all_gather(normed, 'z', axis=0, tiled=True), 'core', a...  20.7 us
    pallas_call x1, Pallas kernels, attend_all(): pl.pallas_call(attend_kernel, grid=(span // Q_BLOCK,), in_specs=[pl.Block...  19.3 us
    all_to_all x1, starting transfers between devices, per_device(): lax.all_to_all(heads_out, ('core', 'z'), split_axis=0, concat_axis=1, til...  16.9 us
  transfers between devices with their start and end apart: 11, of which 7 were waited for; matrix products, arithmetic and copies ran while one was open for 17% of the time, Pallas kernels for 5%

profile of v2, /device:TPU:101, one launch (start us, length us, event | category | flops | bytes accessed | tf_op | source)
XLA Modules:
  0.0 406.1 jit_solution(13169837510767336694)
XLA Ops:
  6.5 1.4 fusion.21
  7.9 2.0 fusion.23
  10.0 30.0 %all-gather.5.cloned.1.call-done = bf16[512,2048]{1,0:T(8,128)(2,1)} async-done(((bf16[128,2048]{1,0:T(8,128)(2,1)}), bf16[512,2048]{1,0:T(8,128)(2,1)}) %all-gather.5.cloned.1.call-update) | async-done | bytes 2097168 | tf_op jit(solution)/shard_map/all_gather | solution.py:182
  40.1 20.7 %all-gather.7.cloned.1.call-done = bf16[1024,2048]{1,0:T(8,128)(2,1)} async-done(((bf16[512,2048]{1,0:T(8,128)(2,1)}), bf16[1024,2048]{1,0:T(8,128)(2,1)}) %all-gather.7.cloned.1.call-update) | async-done | bytes 4194320 | tf_op jit(solution)/shard_map/all_gather | solution.py:181
  60.9 48.6 %all-gather.9.cloned.1.call-done = bf16[1024,2048]{1,0:T(8,128)(2,1)} async-done(((bf16[256,2048]{1,0:T(8,128)(2,1)}), bf16[1024,2048]{1,0:T(8,128)(2,1)}) %all-gather.9.cloned.1.call-update) | async-done | bytes 4194320 | tf_op jit(solution)/shard_map/all_gather | solution.py:186
  109.6 2.1 constant_dynamic-slice_fusion
  111.7 3.8 copy.85
  115.6 6.8 %all-to-all-start = ((bf16[16,64,576]{2,1,0:T(8,128)(2,1)}), bf16[16,64,576]{2,1,0:T(8,128)(2,1)S(1)}, u32[]{:S(2)}, u32[]{:S(2)}) async-start(bf16[16,64,576]{2,1,0:T(8,128)(2,1)} %copy.85), calls=%async_computation | async-start | bytes 2621440 | tf_op jit(solution)/shard_map/all_to_all | solution.py:204
  122.8 15.8 %all-to-all-done = bf16[16,64,576]{2,1,0:T(8,128)(2,1)S(1)} async-done(((bf16[16,64,576]{2,1,0:T(8,128)(2,1)}), bf16[16,64,576]{2,1,0:T(8,128)(2,1)S(1)}, u32[]{:S(2)}, u32[]{:S(2)}) %all-to-all-start) | async-done | bytes 1179680 | tf_op jit(solution)/shard_map/all_to_all | solution.py:204
  138.6 1.5 copy.72
  140.1 3.1 collective-permute-start
  143.2 1.8 reduce-window.6
  145.0 0.3 slice_reduce_fusion
  145.3 0.6 dynamic_slice.7
  145.9 0.7 add_convert_fusion.3
  146.8 0.7 compare_select_fusion.1.th_ref
  147.5 1.5 copy.76
  148.9 4.5 %fusion.67 = f32[1024,384]{0,1:T(8,128)S(1)} fusion(bf16[1024,2048]{1,0:T(8,128)(2,1)} %all-gather.7.cloned.1.call-done, bf16[2048,384]{1,0:T(8,128)(2,1)} %param.20), kind=kOutput, calls=%fused_computation.134 | convolution fusion | flops 1610612736 | bytes 7340032 | tf_op jit(solution)/shard_map/dot_general | solution.py:50
  153.4 0.9 slice.100
  154.3 0.3 copy.83
  154.7 0.3 copy.84
  155.0 1.2 copy.77.qn_ref
  156.3 6.0 %fusion.68 = f32[1024,576]{1,0:T(8,128)S(1)} fusion(bf16[1024,2048]{1,0:T(8,128)(2,1)} %all-gather.7.cloned.1.call-done, bf16[2048,576]{0,1:T(8,128)(2,1)} %param.21), kind=kOutput, calls=%fused_computation.135 | convolution fusion | flops 2415919104 | bytes 8912896 | tf_op jit(solution)/shard_map/dot_general | solution.py:59
  162.3 2.2 subtract_convert_fusion.2
  164.5 0.4 subtract_convert_fusion
  165.0 0.3 maximum_bitcast_fusion.qr_ref
  165.8 0.5 copy-done.3
  166.3 0.4 copy-done.5
  166.9 11.4 %maximum_maximum_fusion = bf16[3072,576]{1,0:T(8,128)(2,1)S(1)} fusion(bf16[1024,32]{1,0:T(8,128)(2,1)S(1)} %get-tuple-element.12, bf16[1024,32]{1,0:T(8,128)(2,1)S(1)} %get-tuple-element.11, bf16[1024,512]{1,0:T(8,128)(2,1)S(1)} %multiply_convert_fusion, bf16[1024,576]{1,0:T(8,128)(2,1)S(1)} %copy-done.5, bf16[1024,576]{1,0:T(8,128)(2,1)S(1)} %bitcast.64), kind=kLoop, calls=%fused_computation.7 | loop fusion | flops 17694720 | bytes 7077888 | tf_op jit(solution)/shard_map/concatenate | solution.py:214
  178.4 1.8 convolution_convert_fusion.kw_ref
  180.2 19.3 %shard_map.154 = bf16[1024,256]{1,0:T(8,128)(2,1)} custom-call(bf16[1024,256]{1,0:T(8,128)(2,1)S(1)} %copy.77.qn_ref, bf16[2,1024,64]{2,1,0:T(8,128)(2,1)S(1)} %maximum_bitcast_fusion.qr_ref, bf16[3072,512]{1,0:T(8,128)(2,1)S(1)} %convolution_convert_fusion.kw_ref, bf16[3072,64]{1,0:T(8,128)(2,1)S(1)} %maximum_maximum_fusion.1.kr_ref, ...), custom_call_target="tpu_custom_call" | custom-call | tf_op jit(solution)/shard_map/pallas_call | solution.py:123
  199.5 16.9 %all-to-all-start.1 = ((bf16[8,128,256]{2,1,0:T(8,128)(2,1)}), bf16[8,128,256]{2,1,0:T(8,128)(2,1)S(1)}, u32[]{:S(2)}, u32[]{:S(2)}) async-start(bf16[8,128,256]{2,1,0:T(8,128)(2,1)} %bitcast.8), calls=%async_computation.1 | async-start | bytes 1048576 | tf_op jit(solution)/shard_map/all_to_all | solution.py:236
  216.7 0.5 fusion.7
  217.2 6.8 %all-to-all-done.1 = bf16[8,128,256]{2,1,0:T(8,128)(2,1)S(1)} async-done(((bf16[8,128,256]{2,1,0:T(8,128)(2,1)}), bf16[8,128,256]{2,1,0:T(8,128)(2,1)S(1)}, u32[]{:S(2)}, u32[]{:S(2)}) %all-to-all-start.1) | async-done | bytes 524320 | tf_op jit(solution)/shard_map/all_to_all | solution.py:236
  224.0 4.7 %convert_reduce_fusion = f32[128,2048]{1,0:T(8,128)S(1)} fusion(bf16[8,256,2048]{2,1,0:T(8,128)(2,1)} %bitcast.65, bf16[8,128,256]{2,1,0:T(8,128)(2,1)S(1)} %all-to-all-done.1), kind=kOutput, calls=%fused_computation.1 | convolution fusion | flops 1079771136 | bytes 9961472 | tf_op jit(solution)/shard_map/tgc,gcd->gtd/dot_general | solution.py:239
  229.0 3.4 convolution_convert_fusion.1
  232.4 9.3 %all-to-all-start.2 = ((bf16[64,16,2048]{2,1,0:T(8,128)(2,1)}), bf16[64,16,2048]{2,1,0:T(8,128)(2,1)}, u32[]{:S(2)}, u32[]{:S(2)}) async-start(bf16[64,16,2048]{2,1,0:T(8,128)(2,1)} %bitcast.61), calls=%async_computation.2 | async-start | bytes 8388608 | tf_op jit(solution)/shard_map/all_to_all | solution.py:259
  241.7 0.8 collective-permute-start.1
  242.6 56.3 %all-to-all-done.2 = bf16[64,16,2048]{2,1,0:T(8,128)(2,1)} async-done(((bf16[64,16,2048]{2,1,0:T(8,128)(2,1)}), bf16[64,16,2048]{2,1,0:T(8,128)(2,1)}, u32[]{:S(2)}, u32[]{:S(2)}) %all-to-all-start.2) | async-done | bytes 4194336 | tf_op jit(solution)/shard_map/all_to_all | solution.py:259
  298.9 10.6 %fusion.2 = f32[1024,1408]{1,0:T(8,128)S(1)} fusion(bf16[1024,2048]{1,0:T(8,128)(2,1)} %bitcast.13, bf16[1,2048,1408]{2,1,0:T(8,128)(2,1)} %param.28), kind=kOutput, calls=%fused_computation.4 | convolution fusion | flops 5905580032 | bytes 15728640 | tf_op jit(solution)/shard_map/dot_general | solution.py:144
  309.4 3.9 fusion.9
  313.4 10.4 %fusion = f32[1024,1408]{1,0:T(8,128)S(1)} fusion(bf16[1024,2048]{1,0:T(8,128)(2,1)} %bitcast.13, bf16[1,2048,1408]{2,1,0:T(8,128)(2,1)} %collective-permute-done.1), kind=kOutput, calls=%fused_computation.2 | convolution fusion | flops 5905580032 | bytes 15728640 | tf_op jit(solution)/shard_map/dot_general | solution.py:144
  323.8 7.1 %add_convert_fusion = bf16[1024,2048]{1,0:T(8,128)(2,1)} fusion(bf16[1024,2048]{1,0:T(8,128)(2,1)S(1)} %fusion.9, bf16[1,704,2048]{2,1,0:T(8,128)(2,1)} %collective-permute-done.2, f32[1024,1408]{1,0:T(8,128)S(1)} %fusion), kind=kOutput, calls=%fused_computation | convolution fusion | flops 2967601152 | bytes 17563648 | tf_op jit(solution)/shard_map/dot_general | solution.py:147
  331.0 9.5 %all-to-all-start.3 = ((bf16[64,16,2048]{2,1,0:T(8,128)(2,1)}), bf16[64,16,2048]{2,1,0:T(8,128)(2,1)}, u32[]{:S(2)}, u32[]{:S(2)}) async-start(bf16[64,16,2048]{2,1,0:T(8,128)(2,1)} %bitcast.66), calls=%async_computation.3 | async-start | bytes 8388608 | tf_op jit(solution)/shard_map/all_to_all | solution.py:265
  340.5 1.2 select_reduce_fusion
  341.7 50.5 %all-to-all-done.3 = bf16[64,16,2048]{2,1,0:T(8,128)(2,1)} async-done(((bf16[64,16,2048]{2,1,0:T(8,128)(2,1)}), bf16[64,16,2048]{2,1,0:T(8,128)(2,1)}, u32[]{:S(2)}, u32[]{:S(2)}) %all-to-all-start.3) | async-done | bytes 4194336 | tf_op jit(solution)/shard_map/all_to_all | solution.py:265
  392.2 3.2 fusion.42
  395.4 4.0 fusion.12
  (62 shorter events, 2.3 us)
Async XLA Ops:
  6.5 103.0 %copy-start = (bf16[16,128,576]{1,2,0:T(8,128)(2,1)S(1)}, bf16[16,128,576]{1,2,0:T(8,128)(2,1)}, u32[]{:S(2)}) copy-start(bf16[16,128,576]{1,2,0:T(8,128)(2,1)} %param.18) | copy-start | bytes 7077892
  6.5 33.5 %all-gather.5.cloned.1.call-start = ((), (), s32[]{:S(2)}) async-start(), calls=%async_computation.4 | async-start | bytes 2621440 | tf_op jit(solution)/shard_map/all_gather | solution.py:182
  10.0 50.8 %all-gather.7.cloned.1.call-start = ((), (), s32[]{:S(2)}) async-start(), calls=%async_computation.5 | async-start | bytes 6291456 | tf_op jit(solution)/shard_map/all_gather | solution.py:181
  40.1 69.5 %all-gather.9.cloned.1.call-start = ((), (), s32[]{:S(2)}) async-start(), calls=%async_computation.6 | async-start | bytes 5242880 | tf_op jit(solution)/shard_map/all_gather | solution.py:186
  60.9 163.1 %all-gather.11.cloned.1.call-start = ((), (), s32[]{:S(2)}) async-start(), calls=%async_computation.7 | async-start | bytes 12582912 | tf_op jit(solution)/shard_map/all_gather | solution.py:185
  111.7 10.7 %copy-start.7 = (s32[128,6]{0,1:T(8,128)S(1)}, s32[128,6]{0,1:T(8,128)}, u32[]{:S(2)}) copy-start(s32[128,6]{0,1:T(8,128)} %param.26) | copy-start | bytes 9220
  115.6 29.8 %copy-start.14 = (s32[16]{0:T(128)S(1)}, s32[16]{0:T(128)}, u32[]{:S(2)}) copy-start(s32[16]{0:T(128)} %param.17) | copy-start | bytes 196
  115.6 23.0 %all-to-all-start = ((bf16[16,64,576]{2,1,0:T(8,128)(2,1)}), bf16[16,64,576]{2,1,0:T(8,128)(2,1)S(1)}, u32[]{:S(2)}, u32[]{:S(2)}) async-start(bf16[16,64,576]{2,1,0:T(8,128)(2,1)} %copy.85), calls=%async_computation | async-start | bytes 2621440 | tf_op jit(solution)/shard_map/all_to_all | solution.py:204
  138.6 8.0 %copy-start.2 = (bf16[16,64,576]{2,1,0:T(8,128)(2,1)}, bf16[16,64,576]{2,1,0:T(8,128)(2,1)S(1)}, u32[]{:S(2)}) copy-start(bf16[16,64,576]{2,1,0:T(8,128)(2,1)S(1)} %all-to-all-done) | copy-start | bytes 3538948
  140.1 7.4 %collective-permute-start = (bf16[1024,576]{0,1:T(8,128)(2,1)}, bf16[1024,576]{0,1:T(8,128)(2,1)S(1)}, u32[]{:S(2)}, u32[]{:S(2)}) collective-permute-start(bf16[1024,576]{0,1:T(8,128)(2,1)} %copy.72), channel_id=1, source_target_pairs={{0,1},{1,0},{2,3},{3,2},{4,5},{5,4},{6,7},{7,6},{8,9},{9,8},{10,11... | collective-permute-start | bytes 3538952 | tf_op jit(solution)/shard_map/ppermute | solution.py:211
  156.3 6.0 %copy-start.11 = (f32[32]{0:T(128)S(1)}, f32[32]{0:T(128)}, u32[]{:S(2)}) copy-start(f32[32]{0:T(128)} %constant.144.clone) | copy-start | bytes 388
  164.5 1.0 copy-start.10
  164.9 1.3 copy-start.3
  165.0 1.7 copy-start.5
  166.9 11.5 %copy-start.13 = (bf16[512,512]{1,0:T(8,128)(2,1)S(1)}, bf16[512,512]{1,0:T(8,128)(2,1)}, u32[]{:S(2)}) copy-start(bf16[512,512]{1,0:T(8,128)(2,1)} %param.23) | copy-start | bytes 1572868
  199.5 24.5 %all-to-all-start.1 = ((bf16[8,128,256]{2,1,0:T(8,128)(2,1)}), bf16[8,128,256]{2,1,0:T(8,128)(2,1)S(1)}, u32[]{:S(2)}, u32[]{:S(2)}) async-start(bf16[8,128,256]{2,1,0:T(8,128)(2,1)} %bitcast.8), calls=%async_computation.1 | async-start | bytes 1048576 | tf_op jit(solution)/shard_map/all_to_all | solution.py:236
  224.0 4.8 %copy-start.4 = (bf16[128,2048]{1,0:T(8,128)(2,1)S(1)}, bf16[128,2048]{1,0:T(8,128)(2,1)}, u32[]{:S(2)}) copy-start(bf16[128,2048]{1,0:T(8,128)(2,1)} %param.16) | copy-start | bytes 1572868
  224.0 5.0 %copy-start.8 = (f32[2048]{0:T(1024)S(1)}, f32[2048]{0:T(1024)}, u32[]{:S(2)}) copy-start(f32[2048]{0:T(1024)} %param.25) | copy-start | bytes 24580
  232.4 66.5 %all-to-all-start.2 = ((bf16[64,16,2048]{2,1,0:T(8,128)(2,1)}), bf16[64,16,2048]{2,1,0:T(8,128)(2,1)}, u32[]{:S(2)}, u32[]{:S(2)}) async-start(bf16[64,16,2048]{2,1,0:T(8,128)(2,1)} %bitcast.61), calls=%async_computation.2 | async-start | bytes 8388608 | tf_op jit(solution)/shard_map/all_to_all | solution.py:259
  241.7 71.7 %collective-permute-start.1 = (bf16[1,2048,1408]{2,1,0:T(8,128)(2,1)}, bf16[1,2048,1408]{2,1,0:T(8,128)(2,1)}, u32[]{:S(2)}, u32[]{:S(2)}) collective-permute-start(bf16[1,2048,1408]{2,1,0:T(8,128)(2,1)} %param.28), channel_id=1, source_target_pairs={{0,1},{1,0},{2,3},{3,2},{4,5},{5,4},{6,7},{7,6},{8,9},{9,8},{10,11... | collective-permute-start | bytes 17301512 | tf_op jit(solution)/shard_map/ppermute | solution.py:171
  242.5 81.4 %collective-permute-start.2 = (bf16[1,704,2048]{2,1,0:T(8,128)(2,1)}, bf16[1,704,2048]{2,1,0:T(8,128)(2,1)}, u32[]{:S(2)}, u32[]{:S(2)}) collective-permute-start(bf16[1,704,2048]{2,1,0:T(8,128)(2,1)} %param.29), channel_id=1, source_target_pairs={{0,1},{1,0},{2,3},{3,2},{4,5},{5,4},{6,7},{7,6},{8,9},{9,8},{10,11... | collective-permute-start | bytes 8650760 | tf_op jit(solution)/shard_map/ppermute | solution.py:172
  298.9 10.6 %copy-start.12 = (bf16[1,704,2048]{2,1,0:T(8,128)(2,1)S(1)}, bf16[1,704,2048]{2,1,0:T(8,128)(2,1)}, u32[]{:S(2)}) copy-start(bf16[1,704,2048]{2,1,0:T(8,128)(2,1)} %param.29) | copy-start | bytes 8650756
  330.9 9.5 %copy-start.9 = (f32[128,6]{0,1:T(8,128)S(1)}, f32[128,6]{0,1:T(8,128)}, u32[]{:S(2)}) copy-start(f32[128,6]{0,1:T(8,128)} %param.27) | copy-start | bytes 9220
  331.0 61.3 %all-to-all-start.3 = ((bf16[64,16,2048]{2,1,0:T(8,128)(2,1)}), bf16[64,16,2048]{2,1,0:T(8,128)(2,1)}, u32[]{:S(2)}, u32[]{:S(2)}) async-start(bf16[64,16,2048]{2,1,0:T(8,128)(2,1)} %bitcast.66), calls=%async_computation.3 | async-start | bytes 8388608 | tf_op jit(solution)/shard_map/all_to_all | solution.py:265
  392.2 3.2 copy-start.6
  392.2 7.2 %copy-start.1 = (bf16[16,128,576]{1,2,0:T(8,128)(2,1)S(1)}, bf16[16,128,576]{1,2,0:T(8,128)(2,1)}, u32[]{:S(2)}) copy-start(bf16[16,128,576]{1,2,0:T(8,128)(2,1)} %param.18) | copy-start | bytes 7077892
Sparse Core Ops, SparseCore 0:
  10.1 29.8 all-gather.4
  41.7 19.1 all-gather.6
  62.5 46.9 all-gather.8
  111.0 25.4 all-gather.10

commit v3 on v1

--- a/solution.py
+++ b/solution.py
@@ -178,7 +178,13 @@
     local_heads = q_weight.shape[1] // (HN + HR)
     query_width = local_heads * (HN + HR)
     normed = norm_rows(tokens.astype(jnp.float32), attn_gain).astype(jnp.bfloat16)
-    shard_rows = lax.all_gather(normed, HEAD, axis=0, tiled=True)
+    shard_rows = lax.all_to_all(
+        jnp.broadcast_to(normed, (head_count,) + normed.shape),
+        HEAD,
+        split_axis=0,
+        concat_axis=0,
+        tiled=True,
+    ).reshape(head_count * own_rows, D)
     o_src, shard_rows = lax.optimization_barrier((o_weight, shard_rows))
     o_full = lax.all_gather(o_src, HEAD, axis=0, tiled=True)
     positions = length + jnp.arange(shard_rows.shape[0], dtype=jnp.int32)
@@ -258,11 +264,15 @@
         concat_axis=0,
         tiled=True,
     ).reshape(EXPERTS * CAP, D)
-    routed_out = jnp.zeros((own_rows, D), jnp.float32)
-    for k in range(TOPK):
-        pick = (slot_tk[:, k : k + 1] == slot_iota[None, :]).astype(jnp.bfloat16)
-        chosen = jnp.dot(pick, returned, preferred_element_type=jnp.float32)
-        routed_out = routed_out + route_weights[:, k : k + 1] * chosen
+    slot_weights = jnp.sum(
+        jnp.where(slot_tk[:, :, None] == slot_iota[None, None, :], route_weights[:, :, None], 0.0),
+        axis=1,
+    )
+    weights_hi = slot_weights.astype(jnp.bfloat16)
+    weights_lo = (slot_weights - weights_hi.astype(jnp.float32)).astype(jnp.bfloat16)
+    routed_out = jnp.dot(weights_hi, returned, preferred_element_type=jnp.float32) + jnp.dot(
+        weights_lo, returned, preferred_element_type=jnp.float32
+    )
     return (hidden + routed_out).astype(jnp.bfloat16)
 
 

time: 351 us -> 358 us (1.020)
  blocking collectives: 24.2 us -> 75.1 us
  waiting for transfers between devices: 147 us -> 114 us
  matrix products: 71.6 us -> 59.9 us
    all_to_all x0 -> x1, blocking collectives: none -> 51.7 us  [per_device(): lax.all_to_all(jnp.broadcast_to(normed, (head_count,) + normed.shape), HE...]
    all_gather x1 -> x0, waiting for transfers between devices: 31.8 us -> none  [per_device(): shard_rows = lax.all_gather(normed, HEAD, axis=0, tiled=True)]
    dot_general x6 -> x2, matrix products: 19.1 us -> 7.19 us  [the longest x1 3.98 us: per_device(): jnp.dot(weights_lo, returned, preferred_element_type=jnp.float32)]
  transfers between devices with their start and end apart: 8 -> 7, of which waited for: 4 -> 3; matrix products, arithmetic and copies ran while one was open for 19% -> 19% of each run, Pallas kernels for 6% -> 5%
where the time goes in v3:
time: 358 us; the launch traced here: 355 us
  waiting for transfers between devices  114 us (32%)
  blocking collectives  75.1 us (21%)
  matrix products  59.9 us (17%)
  starting transfers between devices  37.3 us (10%)
  other arithmetic  22.9 us (6%)
  Pallas kernels  19.2 us (5%)
  between operations  14 us (4%)
  local copies, waits for them, and re-layouts  12.8 us (4%)
    all_to_all x1, waiting for transfers between devices, per_device(): lax.all_to_all(outgoing.reshape(EXPERTS, CAP, D), ('dp', 'z'), split_axis...  53.8 us
    all_to_all x1, waiting for transfers between devices, per_device(): lax.all_to_all(total.astype(jnp.bfloat16).reshape(EXPERTS, CAP, D), ('dp'...  53.6 us
    all_to_all x1, blocking collectives, per_device(): lax.all_to_all(jnp.broadcast_to(normed, (head_count,) + normed.shape), HE...  51.7 us
    all_to_all x1, blocking collectives, per_device(): lax.all_to_all(lax.dynamic_slice_in_dim(latent_cache, core * quarter, qua...  23.4 us
    dot_general x2, matrix products, expert_half(): mixed_rows = jnp.dot(rows, gate_up, preferred_element_type=jnp.float32)  21 us
    pallas_call x1, Pallas kernels, attend_all(): pl.pallas_call(attend_kernel, grid=(span // Q_BLOCK,), in_specs=[pl.Block...  19.2 us
    all_to_all x1, starting transfers between devices, per_device(): lax.all_to_all(heads_out, HEAD, split_axis=0, concat_axis=1, tiled=True)  16.5 us
    concatenate x1, other arithmetic, per_device(): key_rows = jnp.concatenate([mine, theirs, fresh_keys], axis=0)  11.4 us
  transfers between devices with their start and end apart: 7, of which 3 were waited for; matrix products, arithmetic and copies ran while one was open for 19% of the time, Pallas kernels for 5%

profile of v3, /device:TPU:101, one launch (start us, length us, event | category | flops | bytes accessed | tf_op | source)
XLA Modules:
  0.0 355.3 jit_solution(16423639931966775191)
XLA Ops:
  6.5 1.4 fusion.17
  7.9 1.2 fusion.19
  9.2 0.5 broadcast_in_dim.18
  9.7 51.7 %all_to_all.40 = bf16[8,128,2048]{2,1,0:T(8,128)(2,1)} all-to-all(bf16[8,128,2048]{2,1,0:T(8,128)(2,1)S(1)} %broadcast_in_dim.18), channel_id=1, replica_groups=mesh['dp'=16,'z'=4,'core'=2] {'z','core'}, dimensions={0} | all-to-all | bytes 8388608 | tf_op jit(solution)/shard_map/all_to_all | solution.py:181
  61.4 2.1 constant_dynamic-slice_fusion
  63.5 3.8 %copy.85 = bf16[16,64,576]{2,1,0:T(8,128)(2,1)} copy(bf16[16,64,576]{1,2,0:T(8,128)(2,1)} %constant_dynamic-slice_fusion) | data formatting | bytes 2359296
  67.4 23.4 %all_to_all.41 = bf16[16,64,576]{2,1,0:T(8,128)(2,1)S(1)} all-to-all(bf16[16,64,576]{2,1,0:T(8,128)(2,1)} %copy.85), channel_id=1, replica_groups=mesh['dp'=16,'z'=4,'core'=2] {'dp'}, dimensions={0} | all-to-all | bytes 2359296 | tf_op jit(solution)/shard_map/all_to_all | solution.py:202
  90.8 1.5 copy.72
  92.3 2.5 collective-permute-start
  95.2 1.8 reduce-window.6
  97.0 0.3 slice_reduce_fusion
  97.3 0.6 dynamic_slice.7
  97.9 0.6 add_convert_fusion.3
  98.6 0.7 compare_select_fusion.1.th_ref
  99.2 1.5 copy.76
  100.7 4.6 %fusion.42 = f32[1024,384]{0,1:T(8,128)S(1)} fusion(bf16[1024,2048]{1,0:T(8,128)(2,1)} %bitcast.67, bf16[2048,384]{1,0:T(8,128)(2,1)} %param.20), kind=kOutput, calls=%fused_computation.89 | convolution fusion | flops 1610612736 | bytes 7340032 | tf_op jit(solution)/shard_map/dot_general | solution.py:50
  105.4 0.3 copy.83
  105.8 0.3 copy.84
  106.3 6.1 %fusion.43 = f32[1024,576]{1,0:T(8,128)S(1)} fusion(bf16[1024,2048]{1,0:T(8,128)(2,1)} %bitcast.68, bf16[2048,576]{0,1:T(8,128)(2,1)} %param.21), kind=kOutput, calls=%fused_computation.90 | convolution fusion | flops 2415919104 | bytes 8912896 | tf_op jit(solution)/shard_map/dot_general | solution.py:59
  112.4 2.2 subtract_convert_fusion.2
  114.6 0.4 subtract_convert_fusion
  115.1 0.3 maximum_bitcast_fusion.qr_ref
  115.4 0.2 multiply_reduce_fusion
  115.6 0.2 multiply_convert_fusion
  115.9 0.5 copy-done.3
  116.4 0.4 copy-done.5
  116.8 0.2 maximum_maximum_fusion.1.kr_ref
  117.0 11.4 %maximum_maximum_fusion = bf16[3072,576]{1,0:T(8,128)(2,1)S(1)} fusion(bf16[1024,32]{1,0:T(8,128)(2,1)S(1)} %get-tuple-element.12, bf16[1024,32]{1,0:T(8,128)(2,1)S(1)} %get-tuple-element.11, bf16[1024,512]{1,0:T(8,128)(2,1)S(1)} %multiply_convert_fusion, bf16[1024,576]{1,0:T(8,128)(2,1)S(1)} %copy-done.5, bf16[1024,576]{1,0:T(8,128)(2,1)S(1)} %bitcast.65), kind=kLoop, calls=%fused_computation.7 | loop fusion | flops 17694720 | bytes 7077888 | tf_op jit(solution)/shard_map/concatenate | solution.py:212
  128.5 1.8 convolution_convert_fusion.kw_ref
  130.3 19.2 %shard_map.154 = bf16[1024,256]{1,0:T(8,128)(2,1)} custom-call(bf16[1024,256]{1,0:T(8,128)(2,1)S(1)} %copy.77.qn_ref, bf16[2,1024,64]{2,1,0:T(8,128)(2,1)S(1)} %maximum_bitcast_fusion.qr_ref, bf16[3072,512]{1,0:T(8,128)(2,1)S(1)} %convolution_convert_fusion.kw_ref, bf16[3072,64]{1,0:T(8,128)(2,1)S(1)} %maximum_maximum_fusion.1.kr_ref, ...), custom_call_target="tpu_custom_call" | custom-call | tf_op jit(solution)/shard_map/pallas_call | solution.py:125
  149.5 16.5 %all-to-all-start.2 = ((bf16[8,128,256]{2,1,0:T(8,128)(2,1)}), bf16[8,128,256]{2,1,0:T(8,128)(2,1)S(1)}, u32[]{:S(2)}, u32[]{:S(2)}) async-start(bf16[8,128,256]{2,1,0:T(8,128)(2,1)} %bitcast.9), calls=%async_computation.2 | async-start | bytes 1048576 | tf_op jit(solution)/shard_map/all_to_all | solution.py:233
  166.3 0.5 fusion.7
  166.9 6.7 %all-to-all-done.2 = bf16[8,128,256]{2,1,0:T(8,128)(2,1)S(1)} async-done(((bf16[8,128,256]{2,1,0:T(8,128)(2,1)}), bf16[8,128,256]{2,1,0:T(8,128)(2,1)S(1)}, u32[]{:S(2)}, u32[]{:S(2)}) %all-to-all-start.2) | async-done | bytes 524320 | tf_op jit(solution)/shard_map/all_to_all | solution.py:233
  173.6 4.7 %convert_reduce_fusion = f32[128,2048]{1,0:T(8,128)S(1)} fusion(bf16[8,256,2048]{2,1,0:T(8,128)(2,1)} %bitcast.66, bf16[8,128,256]{2,1,0:T(8,128)(2,1)S(1)} %all-to-all-done.2), kind=kOutput, calls=%fused_computation.1 | convolution fusion | flops 1079771136 | bytes 9961472 | tf_op jit(solution)/shard_map/tgc,gcd->gtd/dot_general | solution.py:234
  178.4 0.2 multiply_reduce_fusion.1
  178.6 3.4 convolution_convert_fusion.1
  182.0 8.8 %all-to-all-start.3 = ((bf16[64,16,2048]{2,1,0:T(8,128)(2,1)}), bf16[64,16,2048]{2,1,0:T(8,128)(2,1)}, u32[]{:S(2)}, u32[]{:S(2)}) async-start(bf16[64,16,2048]{2,1,0:T(8,128)(2,1)} %bitcast.62), calls=%async_computation.3 | async-start | bytes 8388608 | tf_op jit(solution)/shard_map/all_to_all | solution.py:254
  190.8 1.3 collective-permute-start.1
  192.3 53.8 %all-to-all-done.3 = bf16[64,16,2048]{2,1,0:T(8,128)(2,1)} async-done(((bf16[64,16,2048]{2,1,0:T(8,128)(2,1)}), bf16[64,16,2048]{2,1,0:T(8,128)(2,1)}, u32[]{:S(2)}, u32[]{:S(2)}) %all-to-all-start.3) | async-done | bytes 4194336 | tf_op jit(solution)/shard_map/all_to_all | solution.py:254
  246.1 10.6 %fusion.2 = f32[1024,1408]{1,0:T(8,128)S(1)} fusion(bf16[1024,2048]{1,0:T(8,128)(2,1)} %bitcast.14, bf16[1,2048,1408]{2,1,0:T(8,128)(2,1)} %param.28), kind=kOutput, calls=%fused_computation.4 | convolution fusion | flops 5905580032 | bytes 15728640 | tf_op jit(solution)/shard_map/dot_general | solution.py:145
  256.7 3.9 %fusion.9 = bf16[1024,2048]{1,0:T(8,128)(2,1)S(1)} fusion(bf16[1,704,2048]{2,1,0:T(8,128)(2,1)S(1)} %copy-done.12, f32[1024,1408]{1,0:T(8,128)S(1)} %fusion.2), kind=kOutput, calls=%fused_computation.19 | convolution fusion | flops 2957115392 | bytes 13369344 | tf_op jit(solution)/shard_map/dot_general | solution.py:148
  260.6 10.4 %fusion = f32[1024,1408]{1,0:T(8,128)S(1)} fusion(bf16[1024,2048]{1,0:T(8,128)(2,1)} %bitcast.14, bf16[1,2048,1408]{2,1,0:T(8,128)(2,1)} %collective-permute-done.1), kind=kOutput, calls=%fused_computation.2 | convolution fusion | flops 5905580032 | bytes 15728640 | tf_op jit(solution)/shard_map/dot_general | solution.py:145
  271.1 7.1 %add_convert_fusion = bf16[1024,2048]{1,0:T(8,128)(2,1)} fusion(bf16[1024,2048]{1,0:T(8,128)(2,1)S(1)} %fusion.9, bf16[1,704,2048]{2,1,0:T(8,128)(2,1)} %collective-permute-done.2, f32[1024,1408]{1,0:T(8,128)S(1)} %fusion), kind=kOutput, calls=%fused_computation | convolution fusion | flops 2967601152 | bytes 17563648 | tf_op jit(solution)/shard_map/dot_general | solution.py:148
  278.2 8.1 %all-to-all-start.4 = ((bf16[64,16,2048]{2,1,0:T(8,128)(2,1)}), bf16[64,16,2048]{2,1,0:T(8,128)(2,1)}, u32[]{:S(2)}, u32[]{:S(2)}) async-start(bf16[64,16,2048]{2,1,0:T(8,128)(2,1)} %bitcast.69), calls=%async_computation.4 | async-start | bytes 8388608 | tf_op jit(solution)/shard_map/all_to_all | solution.py:260
  286.3 1.2 select_reduce_fusion
  287.5 53.6 %all-to-all-done.4 = bf16[64,16,2048]{2,1,0:T(8,128)(2,1)} async-done(((bf16[64,16,2048]{2,1,0:T(8,128)(2,1)}), bf16[64,16,2048]{2,1,0:T(8,128)(2,1)}, u32[]{:S(2)}, u32[]{:S(2)}) %all-to-all-start.4) | async-done | bytes 4194336 | tf_op jit(solution)/shard_map/all_to_all | solution.py:260
  341.1 3.2 fusion.28
  344.3 4.0 %fusion.12 = bf16[128,2048]{1,0:T(8,128)(2,1)} fusion(f32[128,2048]{1,0:T(8,128)S(1)} %fusion.28, bf16[1024,2048]{1,0:T(8,128)(2,1)} %bitcast.20, f32[128,2048]{1,0:T(8,128)S(1)} %convert_reduce_fusion, bf16[128,2048]{1,0:T(8,128)(2,1)} %param.16, f32[128,1024]{1,0:T(8,128)S(1)} %copy-done.6), kind=kOutput, calls=%fused_computation.23 | convolution fusion | flops 538705920 | bytes 7864320 | tf_op jit(solution)/shard_map/dot_general | solution.py:273
  (53 shorter events, 1.3 us)
Async XLA Ops:
  6.5 54.9 %copy-start = (bf16[16,128,576]{1,2,0:T(8,128)(2,1)S(1)}, bf16[16,128,576]{1,2,0:T(8,128)(2,1)}, u32[]{:S(2)}) copy-start(bf16[16,128,576]{1,2,0:T(8,128)(2,1)} %param.18) | copy-start | bytes 7077892
  6.5 167.1 %all-gather.2.cloned.1.call-start = ((), (), s32[]{:S(2)}) async-start(), calls=%async_computation.5 | async-start | bytes 9437184 | tf_op jit(solution)/shard_map/all_gather | solution.py:189
  67.4 27.4 %copy-start.7 = (s32[128,6]{0,1:T(8,128)S(1)}, s32[128,6]{0,1:T(8,128)}, u32[]{:S(2)}) copy-start(s32[128,6]{0,1:T(8,128)} %param.26) | copy-start | bytes 9220
  67.4 29.9 %copy-start.14 = (s32[16]{0:T(128)S(1)}, s32[16]{0:T(128)}, u32[]{:S(2)}) copy-start(s32[16]{0:T(128)} %param.17) | copy-start | bytes 196
  90.8 7.8 %copy-start.2 = (bf16[16,64,576]{2,1,0:T(8,128)(2,1)}, bf16[16,64,576]{2,1,0:T(8,128)(2,1)S(1)}, u32[]{:S(2)}) copy-start(bf16[16,64,576]{2,1,0:T(8,128)(2,1)S(1)} %all_to_all.41) | copy-start | bytes 3538948
  92.3 7.0 %collective-permute-start = (bf16[1024,576]{0,1:T(8,128)(2,1)}, bf16[1024,576]{0,1:T(8,128)(2,1)S(1)}, u32[]{:S(2)}, u32[]{:S(2)}) collective-permute-start(bf16[1024,576]{0,1:T(8,128)(2,1)} %copy.72), channel_id=1, source_target_pairs={{0,1},{1,0},{2,3},{3,2},{4,5},{5,4},{6,7},{7,6},{8,9},{9,8},{10,11... | collective-permute-start | bytes 3538952 | tf_op jit(solution)/shard_map/ppermute | solution.py:209
  106.3 6.1 %copy-start.11 = (f32[32]{0:T(128)S(1)}, f32[32]{0:T(128)}, u32[]{:S(2)}) copy-start(f32[32]{0:T(128)} %constant.84.clone) | copy-start | bytes 388
  114.6 1.0 copy-start.10
  115.1 1.3 copy-start.3
  115.1 1.7 copy-start.5
  117.0 11.5 %copy-start.13 = (bf16[512,512]{1,0:T(8,128)(2,1)S(1)}, bf16[512,512]{1,0:T(8,128)(2,1)}, u32[]{:S(2)}) copy-start(bf16[512,512]{1,0:T(8,128)(2,1)} %param.23) | copy-start | bytes 1572868
  149.5 24.1 %all-to-all-start.2 = ((bf16[8,128,256]{2,1,0:T(8,128)(2,1)}), bf16[8,128,256]{2,1,0:T(8,128)(2,1)S(1)}, u32[]{:S(2)}, u32[]{:S(2)}) async-start(bf16[8,128,256]{2,1,0:T(8,128)(2,1)} %bitcast.9), calls=%async_computation.2 | async-start | bytes 1048576 | tf_op jit(solution)/shard_map/all_to_all | solution.py:233
  173.6 4.8 %copy-start.4 = (bf16[128,2048]{1,0:T(8,128)(2,1)S(1)}, bf16[128,2048]{1,0:T(8,128)(2,1)}, u32[]{:S(2)}) copy-start(bf16[128,2048]{1,0:T(8,128)(2,1)} %param.16) | copy-start | bytes 1572868
  173.6 5.0 %copy-start.8 = (f32[2048]{0:T(1024)S(1)}, f32[2048]{0:T(1024)}, u32[]{:S(2)}) copy-start(f32[2048]{0:T(1024)} %param.25) | copy-start | bytes 24580
  182.0 64.1 %all-to-all-start.3 = ((bf16[64,16,2048]{2,1,0:T(8,128)(2,1)}), bf16[64,16,2048]{2,1,0:T(8,128)(2,1)}, u32[]{:S(2)}, u32[]{:S(2)}) async-start(bf16[64,16,2048]{2,1,0:T(8,128)(2,1)} %bitcast.62), calls=%async_computation.3 | async-start | bytes 8388608 | tf_op jit(solution)/shard_map/all_to_all | solution.py:254
  190.8 69.8 %collective-permute-start.1 = (bf16[1,2048,1408]{2,1,0:T(8,128)(2,1)}, bf16[1,2048,1408]{2,1,0:T(8,128)(2,1)}, u32[]{:S(2)}, u32[]{:S(2)}) collective-permute-start(bf16[1,2048,1408]{2,1,0:T(8,128)(2,1)} %param.28), channel_id=1, source_target_pairs={{0,1},{1,0},{2,3},{3,2},{4,5},{5,4},{6,7},{7,6},{8,9},{9,8},{10,11... | collective-permute-start | bytes 17301512 | tf_op jit(solution)/shard_map/ppermute | solution.py:172
  192.2 78.9 %collective-permute-start.2 = (bf16[1,704,2048]{2,1,0:T(8,128)(2,1)}, bf16[1,704,2048]{2,1,0:T(8,128)(2,1)}, u32[]{:S(2)}, u32[]{:S(2)}) collective-permute-start(bf16[1,704,2048]{2,1,0:T(8,128)(2,1)} %param.29), channel_id=1, source_target_pairs={{0,1},{1,0},{2,3},{3,2},{4,5},{5,4},{6,7},{7,6},{8,9},{9,8},{10,11... | collective-permute-start | bytes 8650760 | tf_op jit(solution)/shard_map/ppermute | solution.py:173
  246.1 10.6 %copy-start.12 = (bf16[1,704,2048]{2,1,0:T(8,128)(2,1)S(1)}, bf16[1,704,2048]{2,1,0:T(8,128)(2,1)}, u32[]{:S(2)}) copy-start(bf16[1,704,2048]{2,1,0:T(8,128)(2,1)} %param.29) | copy-start | bytes 8650756
  278.2 8.1 %copy-start.9 = (f32[128,6]{0,1:T(8,128)S(1)}, f32[128,6]{0,1:T(8,128)}, u32[]{:S(2)}) copy-start(f32[128,6]{0,1:T(8,128)} %param.27) | copy-start | bytes 9220
  278.2 62.9 %all-to-all-start.4 = ((bf16[64,16,2048]{2,1,0:T(8,128)(2,1)}), bf16[64,16,2048]{2,1,0:T(8,128)(2,1)}, u32[]{:S(2)}, u32[]{:S(2)}) async-start(bf16[64,16,2048]{2,1,0:T(8,128)(2,1)} %bitcast.69), calls=%async_computation.4 | async-start | bytes 8388608 | tf_op jit(solution)/shard_map/all_to_all | solution.py:260
  341.1 3.2 copy-start.6
  341.1 7.2 %copy-start.1 = (bf16[16,128,576]{1,2,0:T(8,128)(2,1)S(1)}, bf16[16,128,576]{1,2,0:T(8,128)(2,1)}, u32[]{:S(2)}) copy-start(bf16[16,128,576]{1,2,0:T(8,128)(2,1)} %param.18) | copy-start | bytes 7077892
Sparse Core Ops, SparseCore 0:
  61.5 49.7 all-gather.1
